TPU v7x, 256 devices: a whole 4x4x8 slice. The times are simulated.
256 devices in a mesh: ctx: 8 (over y, x_hi), ch: 32 (over z, x_lo, core).
Axes of the slice: x: 4 (x_hi: 2, x_lo: 2; x = x_hi * 2 + x_lo), y: 4, z: 8, core: 2. Of those that a mesh axis runs over, the one named last changes fastest.
Arguments:
- gate_act: bfloat16 [4096, 8192], P('ctx', 'ch'), may hold values from -6 to 6
- key_act: bfloat16 [4096, 8192], P('ctx', 'ch'), may hold values from -6 to 6
- value_act: bfloat16 [4096, 8192], P('ctx', 'ch'), may hold values from -6 to 6
- filter_taps: float32 [6144, 8192], P('ctx', 'ch'), may hold values from -2 to 2
- skip_gain: float32 [8192], P('ch'), may hold values from 0.5 to 1.5
- w_out: bfloat16 [8192, 8192], P(None, 'ch'), may hold values from -0.0625 to 0.0625
- span_order: int32 [16], replicated, may hold values from 0 to 15, each once
- decode_order: int32 [8], replicated, may hold values from 0 to 7, each once
Outputs:
- projected: bfloat16 [4096, 8192], P('ctx', 'ch')
- tail: float32 [2048, 8192], P('ctx', 'ch')
Inputs may be any that keep to these rules, and one draw needn't show every extreme that they name: `span_order`: each span number once. `decode_order`: each future block number once.
All inputs are finite; a program needn't handle non-finite values.
Results may differ from a plain program's by a relative error of at most 0.017.
Values may be sent and summed in bfloat16 or wider, within the bound.
No kernel may reach another device: no remote copies, remote signals or barrier semaphores. Data moves between devices by JAX's collectives and lax.ppermute only.
A program may use at most 128 MiB of HBM per device.

v0:
```python
import math

import jax
import jax.numpy as jnp
from jax import lax
from jax.experimental import pallas as pl
from jax.experimental.pallas import tpu as pltpu
from jax.sharding import Mesh, PartitionSpec as P


SPAN = 256

HIGH = lax.Precision.HIGH


def forward_table(length):
    half = length // 2
    rows_idx = lax.broadcasted_iota(jnp.int32, (length, length), 0)
    cols_idx = lax.broadcasted_iota(jnp.int32, (length, length), 1)
    frequency = rows_idx % half
    phase = (frequency * cols_idx % length).astype(jnp.float32) * (2.0 * math.pi / length)
    parity = (1 - 2 * (cols_idx % 2)).astype(jnp.float32)
    table = jnp.where(rows_idx < half, jnp.cos(phase), -jnp.sin(phase))
    return jnp.where(rows_idx == half, parity, table)


def inverse_table(length):
    half = length // 2
    rows_idx = lax.broadcasted_iota(jnp.int32, (half, length), 0)
    cols_idx = lax.broadcasted_iota(jnp.int32, (half, length), 1)
    frequency = cols_idx % half
    phase = (frequency * rows_idx % length).astype(jnp.float32) * (2.0 * math.pi / length)
    weight = jnp.where(frequency == 0, 1.0 / length, 2.0 / length)
    table = jnp.where(cols_idx < half, weight * jnp.cos(phase), -weight * jnp.sin(phase))
    parity = (1 - 2 * (rows_idx % 2)).astype(jnp.float32) / length
    return jnp.where(cols_idx == half, parity, table)


def products(seg2d, span2d, lag_idx, lag_ok, n_targets, width, kt=32):
    half = seg2d.shape[0] // 2
    n_slots = span2d.shape[1] // width
    steps = half // kt

    def kernel(lag_ref, ok_ref, seg_re, seg_im, sp_re, sp_im, out_re, out_im):
        out_re[...] = jnp.zeros_like(out_re)
        out_im[...] = jnp.zeros_like(out_im)

        def operands(a, i, rows):
            off = pl.multiple_of(lag_ref[a * n_slots + i] * width, width)
            own = pl.multiple_of(i * width, width)
            return (
                seg_re[rows, pl.ds(off, width)],
                seg_im[rows, pl.ds(off, width)],
                sp_re[rows, pl.ds(own, width)],
                sp_im[rows, pl.ds(own, width)],
            )

        for a in range(n_targets):
            cols = slice(a * width, (a + 1) * width)

            def step(i, carry, a=a, cols=cols):
                @pl.when(ok_ref[a * n_slots + i] > 0)
                def _():
                    lr, li, rr, ri = operands(a, i, slice(None))
                    out_re[:, cols] += lr * rr - li * ri
                    out_im[:, cols] += lr * ri + li * rr

                return carry

            lax.fori_loop(0, n_slots, step, 0)

        @pl.when(pl.program_id(0) == 0)
        def _():
            for a in range(n_targets):
                cols = slice(a * width, (a + 1) * width)

                def fix(i, acc, a=a):
                    fix_re, fix_im = acc
                    w = ok_ref[a * n_slots + i].astype(jnp.float32)
                    lr, li, rr, ri = operands(a, i, slice(0, 8))
                    cross = li * ri
                    return (fix_re + w * cross, fix_im + w * (cross - lr * ri - li * rr))

                zero = jnp.zeros((8, width), jnp.float32)
                fix_re, fix_im = lax.fori_loop(0, n_slots, fix, (zero, zero))
                out_re[0:1, cols] += fix_re[0:1]
                out_im[0:1, cols] += fix_im[0:1]

    seg_cols = seg2d.shape[1]
    span_cols = span2d.shape[1]
    grid_spec = pltpu.PrefetchScalarGridSpec(
        num_scalar_prefetch=2,
        grid=(steps,),
        in_specs=[
            pl.BlockSpec((kt, seg_cols), lambda i, l, o: (i, 0)),
            pl.BlockSpec((kt, seg_cols), lambda i, l, o: (i + steps, 0)),
            pl.BlockSpec((kt, span_cols), lambda i, l, o: (i, 0)),
            pl.BlockSpec((kt, span_cols), lambda i, l, o: (i + steps, 0)),
        ],
        out_specs=[
            pl.BlockSpec((kt, n_targets * width), lambda i, l, o: (i, 0)),
            pl.BlockSpec((kt, n_targets * width), lambda i, l, o: (i, 0)),
        ],
    )
    out_shape = [jax.ShapeDtypeStruct((half, n_targets * width), jnp.float32)] * 2
    re, im = pl.pallas_call(kernel, grid_spec=grid_spec, out_shape=out_shape)(
        lag_idx, lag_ok, seg2d, seg2d, span2d, span2d)
    return jnp.concatenate([re, im], axis=0)


def swap(x, axis):
    count = lax.axis_size(axis)
    return lax.ppermute(x, axis, [(i, (i + 1) % count) for i in range(count)])


def layer(
    gate_act, key_act, value_act, filter_taps, skip_gain, w_out, span_order, decode_order
):
    width = gate_act.shape[1]
    length = 2 * SPAN
    cycle_size = lax.axis_size("ctx")
    position = lax.axis_index("ctx")
    count_spans = 2 * cycle_size
    count_lags = 3 * cycle_size
    forward = forward_table(length).astype(jnp.bfloat16)
    inverse = inverse_table(length)
    signal = (key_act.astype(jnp.float32) * value_act.astype(jnp.float32)).astype(jnp.bfloat16)

    own = jnp.concatenate([filter_taps.astype(jnp.bfloat16), signal], axis=0)
    parts = [own] + [
        lax.ppermute(own, "ctx", [(i, (i + shift) % cycle_size) for i in range(cycle_size)])
        for shift in range(1, cycle_size)
    ]
    stacked = jnp.stack(parts)
    tap_rows = filter_taps.shape[0]
    per_lag = tap_rows // SPAN
    per_span = signal.shape[0] // SPAN
    blocks = stacked[:, :tap_rows].reshape(cycle_size, per_lag, SPAN, width)
    piece = stacked[:, tap_rows:].reshape(cycle_size, per_span, SPAN, width)

    previous = jnp.roll(blocks[:, per_lag - 1 :], -1, axis=0)
    first_part = (jnp.arange(cycle_size) == position)[:, None, None, None]
    previous = jnp.where(first_part, jnp.zeros_like(previous), previous)
    earlier = jnp.concatenate([previous, blocks[:, : per_lag - 1]], axis=1)
    seg_time = jnp.concatenate(
        [
            blocks.transpose(2, 0, 1, 3),
            jnp.zeros((1, cycle_size, per_lag, width), jnp.bfloat16),
            earlier[:, :, 1:].transpose(2, 0, 1, 3),
        ],
        axis=0,
    ).reshape(length, count_lags * width)
    seg_spec = jnp.dot(forward, seg_time, preferred_element_type=jnp.float32)
    span_time = piece.transpose(2, 0, 1, 3).reshape(SPAN, count_spans * width)
    span_spec = jnp.dot(forward[:, :SPAN], span_time, preferred_element_type=jnp.float32)

    held = jnp.arange(count_spans)
    global_slot = per_span * ((position - held // per_span) % cycle_size) + held % per_span
    held_spans = span_order[global_slot]
    my_spans = lax.dynamic_slice_in_dim(span_order, per_span * position, per_span)
    my_future = count_spans + lax.dynamic_index_in_dim(decode_order, position, keepdims=False)
    targets = jnp.concatenate([my_spans, my_future[None]])
    lags = targets[:, None] - held_spans[None, :]
    valid = (lags >= 0).astype(jnp.int32)
    lag = jnp.maximum(lags, 0)
    column = per_lag * ((position - lag // per_lag) % cycle_size) + lag % per_lag
    totals = products(seg_spec, span_spec, column[:2].reshape(-1), valid[:2].reshape(-1), 2, width)
    blocks_out = jnp.dot(inverse, totals, precision=HIGH, preferred_element_type=jnp.float32)
    conv = jnp.concatenate([blocks_out[:, :width], blocks_out[:, width:]], axis=0)
    tail_totals = products(seg_spec, span_spec, column[2], valid[2], 1, width)
    tail_inverse, tail_totals = lax.optimization_barrier((inverse, tail_totals))
    tail = jnp.dot(tail_inverse, tail_totals, precision=HIGH, preferred_element_type=jnp.float32)
    mixed = (
        gate_act.astype(jnp.float32) * (conv + skip_gain[None, :] * signal.astype(jnp.float32))
    ).astype(jnp.bfloat16)

    count_z = lax.axis_size("z")
    xlo = lax.axis_index("xlo")
    core = lax.axis_index("core")
    w5 = w_out.reshape(count_z, 2, 2, width, w_out.shape[1])
    rows = count_z * 2 * width
    w_own = lax.dynamic_index_in_dim(w5, core, axis=2, keepdims=False).reshape(rows, -1)
    w_other = lax.dynamic_index_in_dim(w5, 1 - core, axis=2, keepdims=False).reshape(rows, -1)

    other = swap(mixed, "xlo")
    pair = jnp.where(
        xlo == 0,
        jnp.concatenate([mixed, other], axis=1),
        jnp.concatenate([other, mixed], axis=1),
    )
    ring = lax.all_gather(pair, "z", axis=1, tiled=True)
    summed = jnp.dot(ring, w_own, preferred_element_type=jnp.float32) + jnp.dot(
        swap(ring, "core"), w_other, preferred_element_type=jnp.float32
    )
    projected = summed.astype(jnp.bfloat16)
    return (projected, tail)


def solution(mesh):
    ch = mesh.shape["ch"]
    fine = Mesh(
        mesh.devices.reshape(mesh.shape["ctx"], ch // 4, 2, 2), ("ctx", "z", "xlo", "core")
    )
    chans = ("z", "xlo", "core")
    in_specs = (
        P("ctx", chans),
        P("ctx", chans),
        P("ctx", chans),
        P("ctx", chans),
        P(chans),
        P(None, chans),
        P(),
        P(),
    )
    out_specs = (P("ctx", chans), P("ctx", chans))
    return jax.shard_map(layer, mesh=fine, in_specs=in_specs, out_specs=out_specs, check_vma=False)
```

profile of v0, /device:TPU:1, one launch (start us, length us, event | category | flops | bytes accessed | tf_op | source)
XLA Modules:
  0.0 241.2 jit_solution(683221779713556361)
XLA Ops:
  9.5 3.6 %collective-permute-start = (bf16[1280,256]{1,0:T(8,128)(2,1)S(1)}, bf16[1280,256]{1,0:T(8,128)(2,1)}, u32[]{:S(2)}, u32[]{:S(2)}) collective-permute-start(bf16[1280,256]{1,0:T(8,128)(2,1)S(1)} %pad_maximum_fusion.2), channel_id=1, source_target_pairs={{0,32},{32,64},{64,96},{96,128},{128,160},{160,192},{192,224},{224... | collective-permute-start | bytes 1966088 | tf_op jit(solution)/shard_map/ppermute | solution.py:131
  14.5 2.0 collective-permute-start.2
  18.0 4.5 %collective-permute-start.4 = (bf16[1280,256]{1,0:T(8,128)(2,1)S(1)}, bf16[1280,256]{1,0:T(8,128)(2,1)S(1)}, u32[]{:S(2)}, u32[]{:S(2)}) collective-permute-start(bf16[1280,256]{1,0:T(8,128)(2,1)S(1)} %pad_maximum_fusion.2), channel_id=1, source_target_pairs={{0,160},{32,192},{64,224},{96,0},{128,32},{160,64},{192,96},{224,1... | collective-permute-start | bytes 1966088 | tf_op jit(solution)/shard_map/ppermute | solution.py:131
  28.2 5.0 %select_convert_fusion = bf16[512,512]{1,0:T(8,128)(2,1)S(1)} fusion(s32[512]{0:T(512)S(1)} %get-tuple-element.18, s32[512]{0:T(512)S(1)} %get-tuple-element.19, s32[512]{0:T(512)S(1)} %get-tuple-element.22, s32[512]{0:T(512)S(1)} %get-tuple-element.23, pred[512]{0:T(512)(128)(4,1)S(1)} %get-tuple-element.25, pred[512]{0:T(512)(128)(4,1)S(1)} %get-tuple-element.20, ...), kind=kLoop, calls=%fused_computation.17 | loop fusion | flops 6029312 | bytes 534528 | tf_op jit(solution)/shard_map/convert_element_type | solution.py:125
  36.6 2.0 bitcast_dynamic-update-slice_fusion.6
  38.6 20.4 %collective-permute-done.1 = bf16[1280,256]{1,0:T(8,128)(2,1)} collective-permute-done((bf16[1280,256]{1,0:T(8,128)(2,1)S(1)}, bf16[1280,256]{1,0:T(8,128)(2,1)}, u32[]{:S(2)}, u32[]{:S(2)}) %collective-permute-start.1) | collective-permute-done | bytes 655392 | tf_op jit(solution)/shard_map/ppermute | solution.py:131
  59.0 2.0 bitcast_dynamic-update-slice_fusion.5
  61.9 12.2 %collective-permute-done.3 = bf16[1280,256]{1,0:T(8,128)(2,1)S(1)} collective-permute-done((bf16[1280,256]{1,0:T(8,128)(2,1)S(1)}, bf16[1280,256]{1,0:T(8,128)(2,1)S(1)}, u32[]{:S(2)}, u32[]{:S(2)}) %collective-permute-start.3) | collective-permute-done | bytes 655392 | tf_op jit(solution)/shard_map/ppermute | solution.py:131
  77.6 2.1 slice.59
  82.0 2.0 fusion
  84.0 4.2 %pad_maximum_fusion = bf16[512,8,3,256]{3,0,2,1:T(8,128)(2,1)} fusion(bf16[255,8,3,256]{3,0,2,1:T(8,128)(2,1)S(1)} %fusion, bf16[256,8,3,256]{3,0,2,1:T(8,128)(2,1)S(1)} %bitcast.47, bf16[512]{0:T(512)(128)(2,1)S(1)} %pad.11.clone), kind=kLoop, calls=%fused_computation.1 | loop fusion | flops 18874368 | bytes 12571648 | tf_op jit(solution)/shard_map/concatenate | solution.py:145
  88.2 8.7 %copy.10 = bf16[512,8,3,256]{0,3,2,1:T(8,128)(2,1)} copy(bf16[512,8,3,256]{3,0,2,1:T(8,128)(2,1)} %pad_maximum_fusion) | data formatting | bytes 12582912 | tf_op jit(solution)/shard_map/concatenate | solution.py:145
  96.9 13.4 %fusion.48.seg_re.seg_im = f32[512,6144]{1,0:T(8,128)} fusion(bf16[512,6144]{0,1:T(8,128)(2,1)} %bitcast.50, s32[512]{0:T(512)S(1)} %get-tuple-element.18, s32[512]{0:T(512)S(1)} %get-tuple-element.19, s32[512]{0:T(512)S(1)} %copy-done.4, s32[512]{0:T(512)S(1)} %copy-done.6, pred[512]{0:T(512)(128)(4,1)S(1)} %copy-done.14, ...), kind=kOutput, calls=%fused_computation.105 | convolution fusion | flops 3227254784 | bytes 18884608 | tf_op jit(solution)/shard_map/dot_general | solution.py:153
  110.3 2.4 %copy.11 = bf16[256,8,2,256]{0,3,2,1:T(8,128)(2,1)} copy(bf16[256,8,2,256]{3,0,2,1:T(8,128)(2,1)S(1)} %bitcast.48) | data formatting | bytes 4194304 | tf_op jit(solution)/shard_map/transpose | solution.py:154
  112.8 6.1 %fusion.17.sp_re.sp_im = f32[512,4096]{1,0:T(8,128)} fusion(bf16[256,4096]{0,1:T(8,128)(2,1)} %bitcast.49, bf16[512,512]{1,0:T(8,128)(2,1)S(1)} %select_convert_fusion), kind=kOutput, calls=%fused_computation.46 | convolution fusion | flops 1073741824 | bytes 10747904 | tf_op jit(solution)/shard_map/dot_general | solution.py:155
  118.9 12.7 %shard_map.95 = (f32[256,512]{1,0:T(8,128)}, f32[256,512]{1,0:T(8,128)}) custom-call(s32[32]{0:T(128)} %reshape.173.lag_ref, s32[32]{0:T(128)} %reshape.174.ok_ref, f32[512,6144]{1,0:T(8,128)} %fusion.48.seg_re.seg_im, f32[512,6144]{1,0:T(8,128)} %fusion.48.seg_re.seg_im, f32[512,4096]{1,0:T(8,128)} %fusion.17.sp_re.sp_im, f32[512,4096]{1,0:T(8,128)} %fusion.17.sp_re.sp_im), custom_call_target="tpu_custom_call" | custom-call | tf_op jit(solution)/shard_map/pallas_call | solution.py:106
  131.6 4.0 %fusion.5 = f32[256,512]{1,0:T(8,128)S(1)} fusion(f32[256,512]{1,0:T(8,128)} %get-tuple-element.9, f32[256,512]{1,0:T(8,128)} %get-tuple-element.8, s32[512]{0:T(512)S(1)} %get-tuple-element.18, s32[512]{0:T(512)S(1)} %get-tuple-element.19, s32[256]{0:T(256)S(1)} %copy-done.1, s32[256]{0:T(256)S(1)} %copy-done.2, pred[256]{0:T(512)(128)(4,1)S(1)} %copy-done.15, ...), kind=kOutput, calls=%fused_computation.13 | convolution fusion | flops 406454272 | bytes 1580800 | tf_op jit(solution)/shard_map/dot_general | solution.py:168
  136.2 4.9 %collective-permute-done.7 = bf16[512,256]{1,0:T(8,128)(2,1)S(1)} collective-permute-done((bf16[512,256]{1,0:T(8,128)(2,1)S(1)}, bf16[512,256]{1,0:T(8,128)(2,1)S(1)}, u32[]{:S(2)}, u32[]{:S(2)}) %collective-permute-start.7) | collective-permute-done | bytes 262176 | tf_op jit(solution)/shard_map/ppermute | solution.py:113
  142.1 64.9 %all-gather.2.cloned.1.call-done = bf16[512,4096]{1,0:T(8,128)(2,1)} async-done(((bf16[512,512]{1,0:T(8,128)(2,1)}), bf16[512,4096]{1,0:T(8,128)(2,1)}) %all-gather.2.cloned.1.call-update) | async-done | bytes 4194320 | tf_op jit(solution)/shard_map/all_gather | solution.py:191
  207.8 3.9 %constant_dynamic-slice_fusion.1 = (bf16[8,2,1,256,256]{4,3,2,1,0:T(8,128)(2,1)S(1)}, bf16[8,2,1,256,256]{4,3,2,1,0:T(8,128)(2,1)}) fusion(bf16[8,2,2,256,256]{4,3,2,1,0:T(8,128)(2,1)} %bitcast.51, s32[]{:T(128)S(6)} %select_n.187, s32[]{:T(128)S(6)} %select_n.188), kind=kLoop, calls=%fused_computation.103 | loop fusion | bytes 8388616 | tf_op jit(solution)/shard_map/jit(dynamic_index_in_dim)/dynamic_slice | solution.py:182
  212.3 2.2 fusion.10
  214.5 11.4 %shard_map.96 = (f32[256,256]{1,0:T(8,128)}, f32[256,256]{1,0:T(8,128)}) custom-call(s32[16]{0:T(128)} %get-tuple-element.29.lag_ref, s32[16]{0:T(128)} %get-tuple-element.28.ok_ref, f32[512,6144]{1,0:T(8,128)} %fusion.48.seg_re.seg_im, f32[512,6144]{1,0:T(8,128)} %fusion.48.seg_re.seg_im, f32[512,4096]{1,0:T(8,128)} %fusion.17.sp_re.sp_im, ...), custom_call_target="tpu_custom_call" | custom-call | tf_op jit(solution)/shard_map/pallas_call | solution.py:106
  228.2 4.1 %fusion.50 = f32[512,256]{1,0:T(8,128)S(1)} fusion(bf16[512,4096]{1,0:T(8,128)(2,1)} %collective-permute-done.8, bf16[4096,256]{1,0:T(8,128)(2,1)} %bitcast.53), kind=kOutput, calls=%fused_computation.107 | convolution fusion | flops 1073741824 | bytes 6815744 | tf_op jit(solution)/shard_map/dot_general | solution.py:192
  232.4 2.0 fusion.1
  (92 shorter events, 25.6 us)
Async XLA Ops:
  7.2 199.8 %all-gather.2.cloned.1.call-start = ((), (), s32[]{:S(2)}) async-start(), calls=%async_computation | async-start | bytes 4718592 | tf_op jit(solution)/shard_map/all_gather | solution.py:191
  9.5 26.0 %collective-permute-start = (bf16[1280,256]{1,0:T(8,128)(2,1)S(1)}, bf16[1280,256]{1,0:T(8,128)(2,1)}, u32[]{:S(2)}, u32[]{:S(2)}) collective-permute-start(bf16[1280,256]{1,0:T(8,128)(2,1)S(1)} %pad_maximum_fusion.2), channel_id=1, source_target_pairs={{0,32},{32,64},{64,96},{96,128},{128,160},{160,192},{192,224},{224... | collective-permute-start | bytes 1966088 | tf_op jit(solution)/shard_map/ppermute | solution.py:131
  13.2 45.8 %collective-permute-start.1 = (bf16[1280,256]{1,0:T(8,128)(2,1)S(1)}, bf16[1280,256]{1,0:T(8,128)(2,1)}, u32[]{:S(2)}, u32[]{:S(2)}) collective-permute-start(bf16[1280,256]{1,0:T(8,128)(2,1)S(1)} %pad_maximum_fusion.2), channel_id=1, source_target_pairs={{0,64},{32,96},{64,128},{96,160},{128,192},{160,224},{192,0},{224,... | collective-permute-start | bytes 1966088 | tf_op jit(solution)/shard_map/ppermute | solution.py:131
  14.5 46.5 %collective-permute-start.2 = (bf16[1280,256]{1,0:T(8,128)(2,1)S(1)}, bf16[1280,256]{1,0:T(8,128)(2,1)S(1)}, u32[]{:S(2)}, u32[]{:S(2)}) collective-permute-start(bf16[1280,256]{1,0:T(8,128)(2,1)S(1)} %pad_maximum_fusion.2), channel_id=1, source_target_pairs={{0,96},{32,128},{64,160},{96,192},{128,224},{160,0},{192,32},{224,... | collective-permute-start | bytes 1966088 | tf_op jit(solution)/shard_map/ppermute | solution.py:131
  16.4 57.6 %collective-permute-start.3 = (bf16[1280,256]{1,0:T(8,128)(2,1)S(1)}, bf16[1280,256]{1,0:T(8,128)(2,1)S(1)}, u32[]{:S(2)}, u32[]{:S(2)}) collective-permute-start(bf16[1280,256]{1,0:T(8,128)(2,1)S(1)} %pad_maximum_fusion.2), channel_id=1, source_target_pairs={{0,128},{32,160},{64,192},{96,224},{128,0},{160,32},{192,64},{224,... | collective-permute-start | bytes 1966088 | tf_op jit(solution)/shard_map/ppermute | solution.py:131
  18.0 57.0 %collective-permute-start.4 = (bf16[1280,256]{1,0:T(8,128)(2,1)S(1)}, bf16[1280,256]{1,0:T(8,128)(2,1)S(1)}, u32[]{:S(2)}, u32[]{:S(2)}) collective-permute-start(bf16[1280,256]{1,0:T(8,128)(2,1)S(1)} %pad_maximum_fusion.2), channel_id=1, source_target_pairs={{0,160},{32,192},{64,224},{96,0},{128,32},{160,64},{192,96},{224,1... | collective-permute-start | bytes 1966088 | tf_op jit(solution)/shard_map/ppermute | solution.py:131
  23.4 9.9 %copy-start.9 = (pred[512]{0:T(512)(128)(4,1)}, pred[512]{0:T(512)(128)(4,1)S(1)}, u32[]{:S(2)}) copy-start(pred[512]{0:T(512)(128)(4,1)S(1)} %get-tuple-element.20) | copy-start | bytes 1540
  23.4 54.3 %copy-start.11 = (pred[512]{0:T(512)(128)(4,1)}, pred[512]{0:T(512)(128)(4,1)S(1)}, u32[]{:S(2)}) copy-start(pred[512]{0:T(512)(128)(4,1)S(1)} %get-tuple-element.21) | copy-start | bytes 1540
  23.4 54.2 %copy-start.13 = (pred[512]{0:T(512)(128)(4,1)}, pred[512]{0:T(512)(128)(4,1)S(1)}, u32[]{:S(2)}) copy-start(pred[512]{0:T(512)(128)(4,1)S(1)} %get-tuple-element.25) | copy-start | bytes 1540
  23.4 54.2 %copy-start.17 = (pred[512]{0:T(512)(128)(4,1)}, pred[512]{0:T(512)(128)(4,1)S(1)}, u32[]{:S(2)}) copy-start(pred[512]{0:T(512)(128)(4,1)S(1)} %get-tuple-element.24) | copy-start | bytes 1540
  28.2 51.5 %copy-start.3 = (s32[512]{0:T(512)}, s32[512]{0:T(512)S(1)}, u32[]{:S(2)}) copy-start(s32[512]{0:T(512)S(1)} %get-tuple-element.22) | copy-start | bytes 6148
  28.2 51.5 %copy-start.5 = (s32[512]{0:T(512)}, s32[512]{0:T(512)S(1)}, u32[]{:S(2)}) copy-start(s32[512]{0:T(512)S(1)} %get-tuple-element.23) | copy-start | bytes 6148
  35.6 40.3 %collective-permute-start.5 = (bf16[1280,256]{1,0:T(8,128)(2,1)S(1)}, bf16[1280,256]{1,0:T(8,128)(2,1)S(1)}, u32[]{:S(2)}, u32[]{:S(2)}) collective-permute-start(bf16[1280,256]{1,0:T(8,128)(2,1)S(1)} %pad_maximum_fusion.2), channel_id=1, source_target_pairs={{0,192},{32,224},{64,0},{96,32},{128,64},{160,96},{192,128},{224,1... | collective-permute-start | bytes 1966088 | tf_op jit(solution)/shard_map/ppermute | solution.py:131
  59.0 17.7 %collective-permute-start.6 = (bf16[1280,256]{1,0:T(8,128)(2,1)S(1)}, bf16[1280,256]{1,0:T(8,128)(2,1)S(1)}, u32[]{:S(2)}, u32[]{:S(2)}) collective-permute-start(bf16[1280,256]{1,0:T(8,128)(2,1)S(1)} %pad_maximum_fusion.2), channel_id=1, source_target_pairs={{0,224},{32,0},{64,32},{96,64},{128,96},{160,128},{192,160},{224,1... | collective-permute-start | bytes 1966088 | tf_op jit(solution)/shard_map/ppermute | solution.py:131
  88.2 8.7 %copy-start.6 = (s32[512]{0:T(512)S(1)}, s32[512]{0:T(512)}, u32[]{:S(2)}) copy-start(s32[512]{0:T(512)} %copy-done.5) | copy-start | bytes 6148
  88.2 8.7 %copy-start.10 = (pred[512]{0:T(512)(128)(4,1)S(1)}, pred[512]{0:T(512)(128)(4,1)}, u32[]{:S(2)}) copy-start(pred[512]{0:T(512)(128)(4,1)} %copy-done.9) | copy-start | bytes 1540
  88.2 8.7 %copy-start.12 = (pred[512]{0:T(512)(128)(4,1)S(1)}, pred[512]{0:T(512)(128)(4,1)}, u32[]{:S(2)}) copy-start(pred[512]{0:T(512)(128)(4,1)} %copy-done.11) | copy-start | bytes 1540
  88.2 8.7 %copy-start.14 = (pred[512]{0:T(512)(128)(4,1)S(1)}, pred[512]{0:T(512)(128)(4,1)}, u32[]{:S(2)}) copy-start(pred[512]{0:T(512)(128)(4,1)} %copy-done.13) | copy-start | bytes 1540
  88.2 8.7 %copy-start.18 = (pred[512]{0:T(512)(128)(4,1)S(1)}, pred[512]{0:T(512)(128)(4,1)}, u32[]{:S(2)}) copy-start(pred[512]{0:T(512)(128)(4,1)} %copy-done.17) | copy-start | bytes 1540
  118.9 12.7 %copy-start.1 = (s32[256]{0:T(256)S(1)}, s32[256]{0:T(256)}, u32[]{:S(2)}) copy-start(s32[256]{0:T(256)} %get-tuple-element.26) | copy-start | bytes 3076
  118.9 12.7 %copy-start.2 = (s32[256]{0:T(256)S(1)}, s32[256]{0:T(256)}, u32[]{:S(2)}) copy-start(s32[256]{0:T(256)} %get-tuple-element.27) | copy-start | bytes 3076
  118.9 12.7 %copy-start.15 = (pred[256]{0:T(512)(128)(4,1)S(1)}, pred[256]{0:T(512)(128)(4,1)}, u32[]{:S(2)}) copy-start(pred[256]{0:T(512)(128)(4,1)} %compare_and_fusion) | copy-start | bytes 772
  135.8 5.3 %collective-permute-start.7 = (bf16[512,256]{1,0:T(8,128)(2,1)S(1)}, bf16[512,256]{1,0:T(8,128)(2,1)S(1)}, u32[]{:S(2)}, u32[]{:S(2)}) collective-permute-start(bf16[512,256]{1,0:T(8,128)(2,1)S(1)} %fusion.16), channel_id=1, source_target_pairs={{0,2},{2,0},{1,3},{3,1},{4,6},{6,4},{5,7},{7,5},{8,10},{10,8},{9,1... | collective-permute-start | bytes 786440 | tf_op jit(solution)/shard_map/ppermute | solution.py:113
  207.0 21.3 %collective-permute-start.8 = (bf16[512,4096]{1,0:T(8,128)(2,1)}, bf16[512,4096]{1,0:T(8,128)(2,1)}, u32[]{:S(2)}, u32[]{:S(2)}) collective-permute-start(bf16[512,4096]{1,0:T(8,128)(2,1)} %all-gather.2.cloned.1.call-done), channel_id=1, source_target_pairs={{0,1},{1,0},{2,3},{3,2},{4,5},{5,4},{6,7},{7,6},{8,9},{9,8},{10,11... | collective-permute-start | bytes 12582920 | tf_op jit(solution)/shard_map/ppermute | solution.py:113
  (5 other events, 25.4 us)
Sparse Core Ops, SparseCore 0:
  142.2 64.7 all-gather.1
where the time goes:
time: 242 us; the launch traced here: 241 us
  waiting for transfers between devices  102 us (42%)
  local copies, waits for them, and re-layouts  32.7 us (14%)
  matrix products  30.7 us (13%)
  Pallas kernels  24.1 us (10%)
  other arithmetic  21 us (9%)
  starting transfers between devices  15.3 us (6%)
  between operations  15 us (6%)
    all_gather x1, waiting for transfers between devices, layer(): ring = lax.all_gather(pair, 'z', axis=1, tiled=True)  64.9 us
    ppermute x7, waiting for transfers between devices, layer(): lax.ppermute(own, 'ctx', [(i, (i + shift) % cycle_size) for i in range(cy...  32.6 us
    pallas_call x2, Pallas kernels, products(): pl.pallas_call(kernel, grid_spec=grid_spec, out_shape=out_shape)  24.1 us
    ppermute x7, starting transfers between devices, layer(): lax.ppermute(own, 'ctx', [(i, (i + shift) % cycle_size) for i in range(cy...  14 us
    dot_general x1, matrix products, layer(): seg_spec = jnp.dot(forward, seg_time, preferred_element_type=jnp.float32)  13.4 us
    concatenate x2, local copies, waits for them, and re-layouts, layer(): jnp.concatenate([blocks.transpose(2, 0, 1, 3), jnp.zeros((1, cycle_size,...  8.68 us
    unnamed x44, local copies, waits for them, and re-layouts  7.56 us
    dot_general x1, matrix products, layer(): jnp.dot(forward[:, :SPAN], span_time, preferred_element_type=jnp.float32)  6.1 us
  transfers between devices with their start and end apart: 10, of which 4 were waited for; matrix products, arithmetic and copies ran while one was open for 12% of the time, Pallas kernels for 5%

commit v1 on v0

--- a/solution.py
+++ b/solution.py
@@ -49,10 +49,10 @@
             off = pl.multiple_of(lag_ref[a * n_slots + i] * width, width)
             own = pl.multiple_of(i * width, width)
             return (
-                seg_re[rows, pl.ds(off, width)],
-                seg_im[rows, pl.ds(off, width)],
-                sp_re[rows, pl.ds(own, width)],
-                sp_im[rows, pl.ds(own, width)],
+                seg_re[rows, pl.ds(off, width)].astype(jnp.float32),
+                seg_im[rows, pl.ds(off, width)].astype(jnp.float32),
+                sp_re[rows, pl.ds(own, width)].astype(jnp.float32),
+                sp_im[rows, pl.ds(own, width)].astype(jnp.float32),
             )
 
         for a in range(n_targets):
@@ -77,11 +77,11 @@
                 def fix(i, acc, a=a):
                     fix_re, fix_im = acc
                     w = ok_ref[a * n_slots + i].astype(jnp.float32)
-                    lr, li, rr, ri = operands(a, i, slice(0, 8))
+                    lr, li, rr, ri = operands(a, i, slice(0, 16))
                     cross = li * ri
                     return (fix_re + w * cross, fix_im + w * (cross - lr * ri - li * rr))
 
-                zero = jnp.zeros((8, width), jnp.float32)
+                zero = jnp.zeros((16, width), jnp.float32)
                 fix_re, fix_im = lax.fori_loop(0, n_slots, fix, (zero, zero))
                 out_re[0:1, cols] += fix_re[0:1]
                 out_im[0:1, cols] += fix_im[0:1]
@@ -150,9 +150,11 @@
         ],
         axis=0,
     ).reshape(length, count_lags * width)
-    seg_spec = jnp.dot(forward, seg_time, preferred_element_type=jnp.float32)
+    seg_spec = jnp.dot(forward, seg_time, preferred_element_type=jnp.float32).astype(jnp.bfloat16)
     span_time = piece.transpose(2, 0, 1, 3).reshape(SPAN, count_spans * width)
-    span_spec = jnp.dot(forward[:, :SPAN], span_time, preferred_element_type=jnp.float32)
+    span_spec = jnp.dot(
+        forward[:, :SPAN], span_time, preferred_element_type=jnp.float32
+    ).astype(jnp.bfloat16)
 
     held = jnp.arange(count_spans)
     global_slot = per_span * ((position - held // per_span) % cycle_size) + held % per_span
@@ -175,20 +177,13 @@
     ).astype(jnp.bfloat16)
 
     count_z = lax.axis_size("z")
-    xlo = lax.axis_index("xlo")
     core = lax.axis_index("core")
     w5 = w_out.reshape(count_z, 2, 2, width, w_out.shape[1])
     rows = count_z * 2 * width
     w_own = lax.dynamic_index_in_dim(w5, core, axis=2, keepdims=False).reshape(rows, -1)
     w_other = lax.dynamic_index_in_dim(w5, 1 - core, axis=2, keepdims=False).reshape(rows, -1)
 
-    other = swap(mixed, "xlo")
-    pair = jnp.where(
-        xlo == 0,
-        jnp.concatenate([mixed, other], axis=1),
-        jnp.concatenate([other, mixed], axis=1),
-    )
-    ring = lax.all_gather(pair, "z", axis=1, tiled=True)
+    ring = lax.all_gather(mixed, ("z", "xlo"), axis=1, tiled=True)
     summed = jnp.dot(ring, w_own, preferred_element_type=jnp.float32) + jnp.dot(
         swap(ring, "core"), w_other, preferred_element_type=jnp.float32
     )

time: 242 us -> 299 us (1.24); the launches traced: 241 us -> 294 us
  waiting for transfers between devices: 102 us -> 151 us
  starting transfers between devices: 15.3 us -> 23.3 us
  Pallas kernels: 24.1 us -> 20.4 us
    all_gather x1, waiting for transfers between devices: 64.9 us -> 118 us  [layer(): ring = lax.all_gather(mixed, ('z', 'xlo'), axis=1, tiled=True)]
    ppermute x2 -> x1, starting transfers between devices: 1.29 us -> 9.3 us  [swap(): return lax.ppermute(x, axis, [(i, (i + 1) % count) for i in range(count)])]
    ppermute x2 -> x1, waiting for transfers between devices: 4.86 us -> 0.01 us  [swap(): return lax.ppermute(x, axis, [(i, (i + 1) % count) for i in range(count)])]
    pallas_call x2, Pallas kernels: 24.1 us -> 20.4 us  [products(): pl.pallas_call(kernel, grid_spec=grid_spec, out_shape=out_shape)]
    unnamed x44 -> x42, local copies, waits for them, and re-layouts: 7.56 us -> 7.58 us
  transfers between devices with their start and end apart: 10 -> 9, of which waited for: 4 -> 3; matrix products, arithmetic and copies ran while one was open for 12% -> 11% of each run, Pallas kernels for 5% -> 3%
where the time goes in v1:
time: 299 us; the launch traced here: 294 us
  waiting for transfers between devices  151 us (51%)
  local copies, waits for them, and re-layouts  32.7 us (11%)
  matrix products  30.8 us (10%)
  starting transfers between devices  23.3 us (8%)
  other arithmetic  20.6 us (7%)
  Pallas kernels  20.4 us (7%)
  between operations  15 us (5%)
    all_gather x1, waiting for transfers between devices, layer(): ring = lax.all_gather(mixed, ('z', 'xlo'), axis=1, tiled=True)  118 us
    ppermute x7, waiting for transfers between devices, layer(): lax.ppermute(own, 'ctx', [(i, (i + shift) % cycle_size) for i in range(cy...  32.5 us
    pallas_call x2, Pallas kernels, products(): pl.pallas_call(kernel, grid_spec=grid_spec, out_shape=out_shape)  20.4 us
    ppermute x7, starting transfers between devices, layer(): lax.ppermute(own, 'ctx', [(i, (i + shift) % cycle_size) for i in range(cy...  14 us
    dot_general x1, matrix products, layer(): jnp.dot(forward, seg_time, preferred_element_type=jnp.float32)  12.5 us
    ppermute x1, starting transfers between devices, swap(): return lax.ppermute(x, axis, [(i, (i + 1) % count) for i in range(count)])  9.3 us
    concatenate x2, local copies, waits for them, and re-layouts, layer(): jnp.concatenate([blocks.transpose(2, 0, 1, 3), jnp.zeros((1, cycle_size,...  8.72 us
    unnamed x42, local copies, waits for them, and re-layouts  7.58 us
  transfers between devices with their start and end apart: 9, of which 3 were waited for; matrix products, arithmetic and copies ran while one was open for 11% of the time, Pallas kernels for 3%

profile of v1, /device:TPU:1, one launch (start us, length us, event | category | flops | bytes accessed | tf_op | source)
XLA Modules:
  0.0 293.7 jit_solution(8441680925091479890)
XLA Ops:
  9.5 3.6 %collective-permute-start = (bf16[1280,256]{1,0:T(8,128)(2,1)S(1)}, bf16[1280,256]{1,0:T(8,128)(2,1)}, u32[]{:S(2)}, u32[]{:S(2)}) collective-permute-start(bf16[1280,256]{1,0:T(8,128)(2,1)S(1)} %pad_maximum_fusion.2), channel_id=1, source_target_pairs={{0,32},{32,64},{64,96},{96,128},{128,160},{160,192},{192,224},{224... | collective-permute-start | bytes 1966088 | tf_op jit(solution)/shard_map/ppermute | solution.py:131
  14.5 2.0 collective-permute-start.2
  18.0 4.5 %collective-permute-start.4 = (bf16[1280,256]{1,0:T(8,128)(2,1)S(1)}, bf16[1280,256]{1,0:T(8,128)(2,1)S(1)}, u32[]{:S(2)}, u32[]{:S(2)}) collective-permute-start(bf16[1280,256]{1,0:T(8,128)(2,1)S(1)} %pad_maximum_fusion.2), channel_id=1, source_target_pairs={{0,160},{32,192},{64,224},{96,0},{128,32},{160,64},{192,96},{224,1... | collective-permute-start | bytes 1966088 | tf_op jit(solution)/shard_map/ppermute | solution.py:131
  28.2 5.0 %select_convert_fusion = bf16[512,512]{1,0:T(8,128)(2,1)S(1)} fusion(s32[512]{0:T(512)S(1)} %get-tuple-element.18, s32[512]{0:T(512)S(1)} %get-tuple-element.19, s32[512]{0:T(512)S(1)} %get-tuple-element.22, s32[512]{0:T(512)S(1)} %get-tuple-element.23, pred[512]{0:T(512)(128)(4,1)S(1)} %get-tuple-element.25, pred[512]{0:T(512)(128)(4,1)S(1)} %get-tuple-element.20, ...), kind=kLoop, calls=%fused_computation.19 | loop fusion | flops 6029312 | bytes 534528 | tf_op jit(solution)/shard_map/convert_element_type | solution.py:125
  36.7 2.0 bitcast_dynamic-update-slice_fusion.6
  38.7 20.3 %collective-permute-done.1 = bf16[1280,256]{1,0:T(8,128)(2,1)} collective-permute-done((bf16[1280,256]{1,0:T(8,128)(2,1)S(1)}, bf16[1280,256]{1,0:T(8,128)(2,1)}, u32[]{:S(2)}, u32[]{:S(2)}) %collective-permute-start.1) | collective-permute-done | bytes 655392 | tf_op jit(solution)/shard_map/ppermute | solution.py:131
  59.0 2.0 bitcast_dynamic-update-slice_fusion.5
  61.9 12.2 %collective-permute-done.3 = bf16[1280,256]{1,0:T(8,128)(2,1)S(1)} collective-permute-done((bf16[1280,256]{1,0:T(8,128)(2,1)S(1)}, bf16[1280,256]{1,0:T(8,128)(2,1)S(1)}, u32[]{:S(2)}, u32[]{:S(2)}) %collective-permute-start.3) | collective-permute-done | bytes 655392 | tf_op jit(solution)/shard_map/ppermute | solution.py:131
  77.7 2.1 slice.59
  82.0 2.0 fusion
  84.0 4.2 %pad_maximum_fusion = bf16[512,8,3,256]{3,0,2,1:T(8,128)(2,1)} fusion(bf16[255,8,3,256]{3,0,2,1:T(8,128)(2,1)S(1)} %fusion, bf16[256,8,3,256]{3,0,2,1:T(8,128)(2,1)S(1)} %bitcast.47, bf16[512]{0:T(512)(128)(2,1)S(1)} %pad.7.clone), kind=kLoop, calls=%fused_computation.2 | loop fusion | flops 18874368 | bytes 12571648 | tf_op jit(solution)/shard_map/concatenate | solution.py:145
  88.2 8.7 %copy.10 = bf16[512,8,3,256]{0,3,2,1:T(8,128)(2,1)} copy(bf16[512,8,3,256]{3,0,2,1:T(8,128)(2,1)} %pad_maximum_fusion) | data formatting | bytes 12582912 | tf_op jit(solution)/shard_map/concatenate | solution.py:145
  97.0 12.5 %convolution_convert_fusion.seg_re.seg_im = bf16[512,6144]{1,0:T(8,128)(2,1)} fusion(bf16[512,6144]{0,1:T(8,128)(2,1)} %bitcast.50, s32[512]{0:T(512)S(1)} %get-tuple-element.18, s32[512]{0:T(512)S(1)} %get-tuple-element.19, s32[512]{0:T(512)S(1)} %copy-done.4, s32[512]{0:T(512)S(1)} %copy-done.6, pred[512]{0:T(512)(128)(4,1)S(1)} %copy-done.14, ...), kind=kOutput, calls=%fused_computation.1 | convolution fusion | flops 3230400512 | bytes 12593152 | tf_op jit(solution)/shard_map/dot_general | solution.py:153
  109.5 2.4 copy.11
  111.9 5.0 %convolution_convert_fusion.1.sp_re.sp_im = bf16[512,4096]{1,0:T(8,128)(2,1)} fusion(bf16[256,4096]{0,1:T(8,128)(2,1)} %bitcast.49, bf16[512,512]{1,0:T(8,128)(2,1)S(1)} %select_convert_fusion), kind=kOutput, calls=%fused_computation.3 | convolution fusion | flops 1075838976 | bytes 6553600 | tf_op jit(solution)/shard_map/dot_general | solution.py:155
  116.8 10.9 %shard_map.95 = (f32[256,512]{1,0:T(8,128)}, f32[256,512]{1,0:T(8,128)}) custom-call(s32[32]{0:T(128)} %reshape.173.lag_ref, s32[32]{0:T(128)} %reshape.174.ok_ref, bf16[512,6144]{1,0:T(8,128)(2,1)} %convolution_convert_fusion.seg_re.seg_im, bf16[512,6144]{1,0:T(8,128)(2,1)} %convolution_convert_fusion.seg_re.seg_im, ...), custom_call_target="tpu_custom_call" | custom-call | tf_op jit(solution)/shard_map/pallas_call | solution.py:106
  127.7 4.0 %fusion.5 = f32[256,512]{1,0:T(8,128)S(1)} fusion(f32[256,512]{1,0:T(8,128)} %get-tuple-element.9, f32[256,512]{1,0:T(8,128)} %get-tuple-element.8, s32[512]{0:T(512)S(1)} %get-tuple-element.18, s32[512]{0:T(512)S(1)} %get-tuple-element.19, s32[256]{0:T(256)S(1)} %copy-done.1, s32[256]{0:T(256)S(1)} %copy-done.2, pred[256]{0:T(512)(128)(4,1)S(1)} %copy-done.15, ...), kind=kOutput, calls=%fused_computation.15 | convolution fusion | flops 406454272 | bytes 1580800 | tf_op jit(solution)/shard_map/dot_general | solution.py:170
  132.6 118.3 %all-gather.2.cloned.1.call-done = bf16[512,4096]{1,0:T(8,128)(2,1)} async-done(((bf16[512,256]{1,0:T(8,128)(2,1)}), bf16[512,4096]{1,0:T(8,128)(2,1)}) %all-gather.2.cloned.1.call-update) | async-done | bytes 4194320 | tf_op jit(solution)/shard_map/all_gather | solution.py:186
  250.9 9.3 %collective-permute-start.7 = (bf16[512,4096]{1,0:T(8,128)(2,1)}, bf16[512,4096]{1,0:T(8,128)(2,1)}, u32[]{:S(2)}, u32[]{:S(2)}) collective-permute-start(bf16[512,4096]{1,0:T(8,128)(2,1)} %all-gather.2.cloned.1.call-done), channel_id=1, source_target_pairs={{0,1},{1,0},{2,3},{3,2},{4,5},{5,4},{6,7},{7,6},{8,9},{9,8},{10,11... | collective-permute-start | bytes 12582920 | tf_op jit(solution)/shard_map/ppermute | solution.py:113
  260.2 3.9 %constant_dynamic-slice_fusion = (bf16[8,2,1,256,256]{4,3,2,1,0:T(8,128)(2,1)S(1)}, bf16[8,2,1,256,256]{4,3,2,1,0:T(8,128)(2,1)}) fusion(bf16[8,2,2,256,256]{4,3,2,1,0:T(8,128)(2,1)} %bitcast.51, s32[]{:T(128)S(6)} %select_n.178, s32[]{:T(128)S(6)} %select_n.177), kind=kLoop, calls=%fused_computation.102 | loop fusion | bytes 8388616 | tf_op jit(solution)/shard_map/jit(dynamic_index_in_dim)/dynamic_slice | solution.py:184
  264.7 2.2 fusion.10
  266.9 9.5 %shard_map.96 = (f32[256,256]{1,0:T(8,128)}, f32[256,256]{1,0:T(8,128)}) custom-call(s32[16]{0:T(128)} %get-tuple-element.29.lag_ref, s32[16]{0:T(128)} %get-tuple-element.28.ok_ref, bf16[512,6144]{1,0:T(8,128)(2,1)} %convolution_convert_fusion.seg_re.seg_im, bf16[512,6144]{1,0:T(8,128)(2,1)} %convolution_convert_fusion.seg_re.seg_im, ...), custom_call_target="tpu_custom_call" | custom-call | tf_op jit(solution)/shard_map/pallas_call | solution.py:106
  278.6 4.1 %fusion.48 = f32[512,256]{1,0:T(8,128)S(1)} fusion(bf16[512,4096]{1,0:T(8,128)(2,1)} %all-gather.2.cloned.1.call-done, bf16[4096,256]{1,0:T(8,128)(2,1)} %bitcast.53), kind=kOutput, calls=%fused_computation.106 | convolution fusion | flops 1073741824 | bytes 6815744 | tf_op jit(solution)/shard_map/dot_general | solution.py:187
  282.7 4.1 %fusion.1 = bf16[512,256]{1,0:T(8,128)(2,1)} fusion(f32[512,256]{1,0:T(8,128)S(1)} %fusion.48, bf16[512,4096]{1,0:T(8,128)(2,1)} %collective-permute-done.7, bf16[4096,256]{1,0:T(8,128)(2,1)S(1)} %bitcast.52), kind=kOutput, calls=%fused_computation.10 | convolution fusion | flops 1074003968 | bytes 7077888 | tf_op jit(solution)/shard_map/dot_general | solution.py:187
  (87 shorter events, 24.0 us)
Async XLA Ops:
  7.2 243.7 %all-gather.2.cloned.1.call-start = ((), (), s32[]{:S(2)}) async-start(), calls=%async_computation | async-start | bytes 4456448 | tf_op jit(solution)/shard_map/all_gather | solution.py:186
  9.5 26.1 %collective-permute-start = (bf16[1280,256]{1,0:T(8,128)(2,1)S(1)}, bf16[1280,256]{1,0:T(8,128)(2,1)}, u32[]{:S(2)}, u32[]{:S(2)}) collective-permute-start(bf16[1280,256]{1,0:T(8,128)(2,1)S(1)} %pad_maximum_fusion.2), channel_id=1, source_target_pairs={{0,32},{32,64},{64,96},{96,128},{128,160},{160,192},{192,224},{224... | collective-permute-start | bytes 1966088 | tf_op jit(solution)/shard_map/ppermute | solution.py:131
  13.2 45.8 %collective-permute-start.1 = (bf16[1280,256]{1,0:T(8,128)(2,1)S(1)}, bf16[1280,256]{1,0:T(8,128)(2,1)}, u32[]{:S(2)}, u32[]{:S(2)}) collective-permute-start(bf16[1280,256]{1,0:T(8,128)(2,1)S(1)} %pad_maximum_fusion.2), channel_id=1, source_target_pairs={{0,64},{32,96},{64,128},{96,160},{128,192},{160,224},{192,0},{224,... | collective-permute-start | bytes 1966088 | tf_op jit(solution)/shard_map/ppermute | solution.py:131
  14.5 46.5 %collective-permute-start.2 = (bf16[1280,256]{1,0:T(8,128)(2,1)S(1)}, bf16[1280,256]{1,0:T(8,128)(2,1)S(1)}, u32[]{:S(2)}, u32[]{:S(2)}) collective-permute-start(bf16[1280,256]{1,0:T(8,128)(2,1)S(1)} %pad_maximum_fusion.2), channel_id=1, source_target_pairs={{0,96},{32,128},{64,160},{96,192},{128,224},{160,0},{192,32},{224,... | collective-permute-start | bytes 1966088 | tf_op jit(solution)/shard_map/ppermute | solution.py:131
  16.4 57.6 %collective-permute-start.3 = (bf16[1280,256]{1,0:T(8,128)(2,1)S(1)}, bf16[1280,256]{1,0:T(8,128)(2,1)S(1)}, u32[]{:S(2)}, u32[]{:S(2)}) collective-permute-start(bf16[1280,256]{1,0:T(8,128)(2,1)S(1)} %pad_maximum_fusion.2), channel_id=1, source_target_pairs={{0,128},{32,160},{64,192},{96,224},{128,0},{160,32},{192,64},{224,... | collective-permute-start | bytes 1966088 | tf_op jit(solution)/shard_map/ppermute | solution.py:131
  18.0 57.0 %collective-permute-start.4 = (bf16[1280,256]{1,0:T(8,128)(2,1)S(1)}, bf16[1280,256]{1,0:T(8,128)(2,1)S(1)}, u32[]{:S(2)}, u32[]{:S(2)}) collective-permute-start(bf16[1280,256]{1,0:T(8,128)(2,1)S(1)} %pad_maximum_fusion.2), channel_id=1, source_target_pairs={{0,160},{32,192},{64,224},{96,0},{128,32},{160,64},{192,96},{224,1... | collective-permute-start | bytes 1966088 | tf_op jit(solution)/shard_map/ppermute | solution.py:131
  23.4 9.9 %copy-start.9 = (pred[512]{0:T(512)(128)(4,1)}, pred[512]{0:T(512)(128)(4,1)S(1)}, u32[]{:S(2)}) copy-start(pred[512]{0:T(512)(128)(4,1)S(1)} %get-tuple-element.20) | copy-start | bytes 1540
  23.4 54.3 %copy-start.11 = (pred[512]{0:T(512)(128)(4,1)}, pred[512]{0:T(512)(128)(4,1)S(1)}, u32[]{:S(2)}) copy-start(pred[512]{0:T(512)(128)(4,1)S(1)} %get-tuple-element.21) | copy-start | bytes 1540
  23.4 54.3 %copy-start.13 = (pred[512]{0:T(512)(128)(4,1)}, pred[512]{0:T(512)(128)(4,1)S(1)}, u32[]{:S(2)}) copy-start(pred[512]{0:T(512)(128)(4,1)S(1)} %get-tuple-element.25) | copy-start | bytes 1540
  23.4 54.3 %copy-start.16 = (pred[512]{0:T(512)(128)(4,1)}, pred[512]{0:T(512)(128)(4,1)S(1)}, u32[]{:S(2)}) copy-start(pred[512]{0:T(512)(128)(4,1)S(1)} %get-tuple-element.24) | copy-start | bytes 1540
  28.2 51.5 %copy-start.3 = (s32[512]{0:T(512)}, s32[512]{0:T(512)S(1)}, u32[]{:S(2)}) copy-start(s32[512]{0:T(512)S(1)} %get-tuple-element.22) | copy-start | bytes 6148
  28.2 51.5 %copy-start.5 = (s32[512]{0:T(512)}, s32[512]{0:T(512)S(1)}, u32[]{:S(2)}) copy-start(s32[512]{0:T(512)S(1)} %get-tuple-element.23) | copy-start | bytes 6148
  35.6 40.2 %collective-permute-start.5 = (bf16[1280,256]{1,0:T(8,128)(2,1)S(1)}, bf16[1280,256]{1,0:T(8,128)(2,1)S(1)}, u32[]{:S(2)}, u32[]{:S(2)}) collective-permute-start(bf16[1280,256]{1,0:T(8,128)(2,1)S(1)} %pad_maximum_fusion.2), channel_id=1, source_target_pairs={{0,192},{32,224},{64,0},{96,32},{128,64},{160,96},{192,128},{224,1... | collective-permute-start | bytes 1966088 | tf_op jit(solution)/shard_map/ppermute | solution.py:131
  59.0 17.7 %collective-permute-start.6 = (bf16[1280,256]{1,0:T(8,128)(2,1)S(1)}, bf16[1280,256]{1,0:T(8,128)(2,1)S(1)}, u32[]{:S(2)}, u32[]{:S(2)}) collective-permute-start(bf16[1280,256]{1,0:T(8,128)(2,1)S(1)} %pad_maximum_fusion.2), channel_id=1, source_target_pairs={{0,224},{32,0},{64,32},{96,64},{128,96},{160,128},{192,160},{224,1... | collective-permute-start | bytes 1966088 | tf_op jit(solution)/shard_map/ppermute | solution.py:131
  88.2 8.7 %copy-start.4 = (s32[512]{0:T(512)S(1)}, s32[512]{0:T(512)}, u32[]{:S(2)}) copy-start(s32[512]{0:T(512)} %copy-done.3) | copy-start | bytes 6148
  88.2 8.7 %copy-start.6 = (s32[512]{0:T(512)S(1)}, s32[512]{0:T(512)}, u32[]{:S(2)}) copy-start(s32[512]{0:T(512)} %copy-done.5) | copy-start | bytes 6148
  88.2 8.7 %copy-start.10 = (pred[512]{0:T(512)(128)(4,1)S(1)}, pred[512]{0:T(512)(128)(4,1)}, u32[]{:S(2)}) copy-start(pred[512]{0:T(512)(128)(4,1)} %copy-done.9) | copy-start | bytes 1540
  88.2 8.7 %copy-start.12 = (pred[512]{0:T(512)(128)(4,1)S(1)}, pred[512]{0:T(512)(128)(4,1)}, u32[]{:S(2)}) copy-start(pred[512]{0:T(512)(128)(4,1)} %copy-done.11) | copy-start | bytes 1540
  88.2 8.8 %copy-start.14 = (pred[512]{0:T(512)(128)(4,1)S(1)}, pred[512]{0:T(512)(128)(4,1)}, u32[]{:S(2)}) copy-start(pred[512]{0:T(512)(128)(4,1)} %copy-done.13) | copy-start | bytes 1540
  88.2 8.8 %copy-start.17 = (pred[512]{0:T(512)(128)(4,1)S(1)}, pred[512]{0:T(512)(128)(4,1)}, u32[]{:S(2)}) copy-start(pred[512]{0:T(512)(128)(4,1)} %copy-done.16) | copy-start | bytes 1540
  116.8 10.9 %copy-start.1 = (s32[256]{0:T(256)S(1)}, s32[256]{0:T(256)}, u32[]{:S(2)}) copy-start(s32[256]{0:T(256)} %get-tuple-element.26) | copy-start | bytes 3076
  116.8 10.9 %copy-start.2 = (s32[256]{0:T(256)S(1)}, s32[256]{0:T(256)}, u32[]{:S(2)}) copy-start(s32[256]{0:T(256)} %get-tuple-element.27) | copy-start | bytes 3076
  116.8 10.9 %copy-start.15 = (pred[256]{0:T(512)(128)(4,1)S(1)}, pred[256]{0:T(512)(128)(4,1)}, u32[]{:S(2)}) copy-start(pred[256]{0:T(512)(128)(4,1)} %compare_and_fusion) | copy-start | bytes 772
  250.9 31.8 %collective-permute-start.7 = (bf16[512,4096]{1,0:T(8,128)(2,1)}, bf16[512,4096]{1,0:T(8,128)(2,1)}, u32[]{:S(2)}, u32[]{:S(2)}) collective-permute-start(bf16[512,4096]{1,0:T(8,128)(2,1)} %all-gather.2.cloned.1.call-done), channel_id=1, source_target_pairs={{0,1},{1,0},{2,3},{3,2},{4,5},{5,4},{6,7},{7,6},{8,9},{9,8},{10,11... | collective-permute-start | bytes 12582920 | tf_op jit(solution)/shard_map/ppermute | solution.py:113
  (3 other events, 10.2 us)
Sparse Core Ops, SparseCore 0:
  132.8 118.0 all-gather.1

commit v2 on v1

--- a/solution.py
+++ b/solution.py
@@ -9,6 +9,7 @@
 
 
 SPAN = 256
+
 
 HIGH = lax.Precision.HIGH
 
@@ -177,13 +178,20 @@
     ).astype(jnp.bfloat16)
 
     count_z = lax.axis_size("z")
+    xlo = lax.axis_index("xlo")
     core = lax.axis_index("core")
     w5 = w_out.reshape(count_z, 2, 2, width, w_out.shape[1])
     rows = count_z * 2 * width
     w_own = lax.dynamic_index_in_dim(w5, core, axis=2, keepdims=False).reshape(rows, -1)
     w_other = lax.dynamic_index_in_dim(w5, 1 - core, axis=2, keepdims=False).reshape(rows, -1)
 
-    ring = lax.all_gather(mixed, ("z", "xlo"), axis=1, tiled=True)
+    other = swap(mixed, "xlo")
+    pair = jnp.where(
+        xlo == 0,
+        jnp.concatenate([mixed, other], axis=1),
+        jnp.concatenate([other, mixed], axis=1),
+    )
+    ring = lax.all_gather(pair, "z", axis=1, tiled=True)
     summed = jnp.dot(ring, w_own, preferred_element_type=jnp.float32) + jnp.dot(
         swap(ring, "core"), w_other, preferred_element_type=jnp.float32
     )

time: 299 us -> 236 us (0.79); the launches traced: 294 us -> 235 us
  waiting for transfers between devices: 151 us -> 102 us
  starting transfers between devices: 23.3 us -> 15.3 us
    all_gather x1, waiting for transfers between devices: 118 us -> 65 us  [layer(): ring = lax.all_gather(pair, 'z', axis=1, tiled=True)]
    ppermute x1 -> x2, starting transfers between devices: 9.3 us -> 1.3 us  [swap(): return lax.ppermute(x, axis, [(i, (i + 1) % count) for i in range(count)])]
    ppermute x1 -> x2, waiting for transfers between devices: 0.01 us -> 4.85 us  [swap(): return lax.ppermute(x, axis, [(i, (i + 1) % count) for i in range(count)])]
    unnamed x42 -> x44, local copies, waits for them, and re-layouts: 7.58 us -> 7.56 us
  transfers between devices with their start and end apart: 9 -> 10, of which waited for: 3 -> 4; matrix products, arithmetic and copies ran while one was open for 11% -> 12% of each run, Pallas kernels for 3% -> 4%
where the time goes in v2:
time: 236 us; the launch traced here: 235 us
  waiting for transfers between devices  102 us (43%)
  local copies, waits for them, and re-layouts  32.7 us (14%)
  matrix products  28.6 us (12%)
  other arithmetic  20.9 us (9%)
  Pallas kernels  20.4 us (9%)
  starting transfers between devices  15.3 us (6%)
  between operations  15 us (6%)
    all_gather x1, waiting for transfers between devices, layer(): ring = lax.all_gather(pair, 'z', axis=1, tiled=True)  65 us
    ppermute x7, waiting for transfers between devices, layer(): lax.ppermute(own, 'ctx', [(i, (i + shift) % cycle_size) for i in range(cy...  32.6 us
    pallas_call x2, Pallas kernels, products(): pl.pallas_call(kernel, grid_spec=grid_spec, out_shape=out_shape)  20.4 us
    ppermute x7, starting transfers between devices, layer(): lax.ppermute(own, 'ctx', [(i, (i + shift) % cycle_size) for i in range(cy...  14 us
    dot_general x1, matrix products, layer(): jnp.dot(forward, seg_time, preferred_element_type=jnp.float32)  12.5 us
    concatenate x2, local copies, waits for them, and re-layouts, layer(): jnp.concatenate([blocks.transpose(2, 0, 1, 3), jnp.zeros((1, cycle_size,...  8.71 us
    unnamed x44, local copies, waits for them, and re-layouts  7.56 us
    convert_element_type x1, other arithmetic, layer(): forward = forward_table(length).astype(jnp.bfloat16)  5.02 us
  transfers between devices with their start and end apart: 10, of which 4 were waited for; matrix products, arithmetic and copies ran while one was open for 12% of the time, Pallas kernels for 4%

profile of v2, /device:TPU:1, one launch (start us, length us, event | category | flops | bytes accessed | tf_op | source)
XLA Modules:
  0.0 235.4 jit_solution(16704088072061165759)
XLA Ops:
  9.5 3.6 %collective-permute-start = (bf16[1280,256]{1,0:T(8,128)(2,1)S(1)}, bf16[1280,256]{1,0:T(8,128)(2,1)}, u32[]{:S(2)}, u32[]{:S(2)}) collective-permute-start(bf16[1280,256]{1,0:T(8,128)(2,1)S(1)} %pad_maximum_fusion.2), channel_id=1, source_target_pairs={{0,32},{32,64},{64,96},{96,128},{128,160},{160,192},{192,224},{224... | collective-permute-start | bytes 1966088 | tf_op jit(solution)/shard_map/ppermute | solution.py:132
  14.5 2.0 collective-permute-start.2
  18.0 4.5 %collective-permute-start.4 = (bf16[1280,256]{1,0:T(8,128)(2,1)S(1)}, bf16[1280,256]{1,0:T(8,128)(2,1)S(1)}, u32[]{:S(2)}, u32[]{:S(2)}) collective-permute-start(bf16[1280,256]{1,0:T(8,128)(2,1)S(1)} %pad_maximum_fusion.2), channel_id=1, source_target_pairs={{0,160},{32,192},{64,224},{96,0},{128,32},{160,64},{192,96},{224,1... | collective-permute-start | bytes 1966088 | tf_op jit(solution)/shard_map/ppermute | solution.py:132
  28.2 5.0 %select_convert_fusion = bf16[512,512]{1,0:T(8,128)(2,1)S(1)} fusion(s32[512]{0:T(512)S(1)} %get-tuple-element.18, s32[512]{0:T(512)S(1)} %get-tuple-element.19, s32[512]{0:T(512)S(1)} %get-tuple-element.22, s32[512]{0:T(512)S(1)} %get-tuple-element.23, pred[512]{0:T(512)(128)(4,1)S(1)} %get-tuple-element.25, pred[512]{0:T(512)(128)(4,1)S(1)} %get-tuple-element.20, ...), kind=kLoop, calls=%fused_computation.19 | loop fusion | flops 6029312 | bytes 534528 | tf_op jit(solution)/shard_map/convert_element_type | solution.py:126
  36.6 2.0 bitcast_dynamic-update-slice_fusion.6
  38.6 20.4 %collective-permute-done.1 = bf16[1280,256]{1,0:T(8,128)(2,1)} collective-permute-done((bf16[1280,256]{1,0:T(8,128)(2,1)S(1)}, bf16[1280,256]{1,0:T(8,128)(2,1)}, u32[]{:S(2)}, u32[]{:S(2)}) %collective-permute-start.1) | collective-permute-done | bytes 655392 | tf_op jit(solution)/shard_map/ppermute | solution.py:132
  59.0 2.0 bitcast_dynamic-update-slice_fusion.5
  61.9 12.2 %collective-permute-done.3 = bf16[1280,256]{1,0:T(8,128)(2,1)S(1)} collective-permute-done((bf16[1280,256]{1,0:T(8,128)(2,1)S(1)}, bf16[1280,256]{1,0:T(8,128)(2,1)S(1)}, u32[]{:S(2)}, u32[]{:S(2)}) %collective-permute-start.3) | collective-permute-done | bytes 655392 | tf_op jit(solution)/shard_map/ppermute | solution.py:132
  77.6 2.1 slice.59
  82.0 2.0 fusion
  84.0 4.2 %pad_maximum_fusion = bf16[512,8,3,256]{3,0,2,1:T(8,128)(2,1)} fusion(bf16[255,8,3,256]{3,0,2,1:T(8,128)(2,1)S(1)} %fusion, bf16[256,8,3,256]{3,0,2,1:T(8,128)(2,1)S(1)} %bitcast.47, bf16[512]{0:T(512)(128)(2,1)S(1)} %pad.11.clone), kind=kLoop, calls=%fused_computation.2 | loop fusion | flops 18874368 | bytes 12571648 | tf_op jit(solution)/shard_map/concatenate | solution.py:146
  88.2 8.7 %copy.10 = bf16[512,8,3,256]{0,3,2,1:T(8,128)(2,1)} copy(bf16[512,8,3,256]{3,0,2,1:T(8,128)(2,1)} %pad_maximum_fusion) | data formatting | bytes 12582912 | tf_op jit(solution)/shard_map/concatenate | solution.py:146
  96.9 12.5 %convolution_convert_fusion.seg_re.seg_im = bf16[512,6144]{1,0:T(8,128)(2,1)} fusion(bf16[512,6144]{0,1:T(8,128)(2,1)} %bitcast.50, s32[512]{0:T(512)S(1)} %get-tuple-element.18, s32[512]{0:T(512)S(1)} %get-tuple-element.19, s32[512]{0:T(512)S(1)} %copy-done.4, s32[512]{0:T(512)S(1)} %copy-done.6, pred[512]{0:T(512)(128)(4,1)S(1)} %copy-done.14, ...), kind=kOutput, calls=%fused_computation.1 | convolution fusion | flops 3230400512 | bytes 12593152 | tf_op jit(solution)/shard_map/dot_general | solution.py:154
  109.4 2.4 %copy.11 = bf16[256,8,2,256]{0,3,2,1:T(8,128)(2,1)} copy(bf16[256,8,2,256]{3,0,2,1:T(8,128)(2,1)S(1)} %bitcast.48) | data formatting | bytes 4194304 | tf_op jit(solution)/shard_map/transpose | solution.py:155
  111.8 5.0 %convolution_convert_fusion.1.sp_re.sp_im = bf16[512,4096]{1,0:T(8,128)(2,1)} fusion(bf16[256,4096]{0,1:T(8,128)(2,1)} %bitcast.49, bf16[512,512]{1,0:T(8,128)(2,1)S(1)} %select_convert_fusion), kind=kOutput, calls=%fused_computation.3 | convolution fusion | flops 1075838976 | bytes 6553600 | tf_op jit(solution)/shard_map/dot_general | solution.py:156
  116.8 10.9 %shard_map.95 = (f32[256,512]{1,0:T(8,128)}, f32[256,512]{1,0:T(8,128)}) custom-call(s32[32]{0:T(128)} %reshape.173.lag_ref, s32[32]{0:T(128)} %reshape.174.ok_ref, bf16[512,6144]{1,0:T(8,128)(2,1)} %convolution_convert_fusion.seg_re.seg_im, bf16[512,6144]{1,0:T(8,128)(2,1)} %convolution_convert_fusion.seg_re.seg_im, ...), custom_call_target="tpu_custom_call" | custom-call | tf_op jit(solution)/shard_map/pallas_call | solution.py:107
  127.7 4.0 %fusion.5 = f32[256,512]{1,0:T(8,128)S(1)} fusion(f32[256,512]{1,0:T(8,128)} %get-tuple-element.9, f32[256,512]{1,0:T(8,128)} %get-tuple-element.8, s32[512]{0:T(512)S(1)} %get-tuple-element.18, s32[512]{0:T(512)S(1)} %get-tuple-element.19, s32[256]{0:T(256)S(1)} %copy-done.1, s32[256]{0:T(256)S(1)} %copy-done.2, pred[256]{0:T(512)(128)(4,1)S(1)} %copy-done.15, ...), kind=kOutput, calls=%fused_computation.15 | convolution fusion | flops 406454272 | bytes 1580800 | tf_op jit(solution)/shard_map/dot_general | solution.py:171
  132.3 4.8 %collective-permute-done.7 = bf16[512,256]{1,0:T(8,128)(2,1)S(1)} collective-permute-done((bf16[512,256]{1,0:T(8,128)(2,1)S(1)}, bf16[512,256]{1,0:T(8,128)(2,1)S(1)}, u32[]{:S(2)}, u32[]{:S(2)}) %collective-permute-start.7) | collective-permute-done | bytes 262176 | tf_op jit(solution)/shard_map/ppermute | solution.py:114
  138.1 65.0 %all-gather.2.cloned.1.call-done = bf16[512,4096]{1,0:T(8,128)(2,1)} async-done(((bf16[512,512]{1,0:T(8,128)(2,1)}), bf16[512,4096]{1,0:T(8,128)(2,1)}) %all-gather.2.cloned.1.call-update) | async-done | bytes 4194320 | tf_op jit(solution)/shard_map/all_gather | solution.py:194
  204.0 3.9 %constant_dynamic-slice_fusion.1 = (bf16[8,2,1,256,256]{4,3,2,1,0:T(8,128)(2,1)S(1)}, bf16[8,2,1,256,256]{4,3,2,1,0:T(8,128)(2,1)}) fusion(bf16[8,2,2,256,256]{4,3,2,1,0:T(8,128)(2,1)} %bitcast.51, s32[]{:T(128)S(6)} %select_n.187, s32[]{:T(128)S(6)} %select_n.188), kind=kLoop, calls=%fused_computation.104 | loop fusion | bytes 8388616 | tf_op jit(solution)/shard_map/jit(dynamic_index_in_dim)/dynamic_slice | solution.py:185
  208.5 2.2 fusion.10
  210.6 9.5 %shard_map.96 = (f32[256,256]{1,0:T(8,128)}, f32[256,256]{1,0:T(8,128)}) custom-call(s32[16]{0:T(128)} %get-tuple-element.29.lag_ref, s32[16]{0:T(128)} %get-tuple-element.28.ok_ref, bf16[512,6144]{1,0:T(8,128)(2,1)} %convolution_convert_fusion.seg_re.seg_im, bf16[512,6144]{1,0:T(8,128)(2,1)} %convolution_convert_fusion.seg_re.seg_im, ...), custom_call_target="tpu_custom_call" | custom-call | tf_op jit(solution)/shard_map/pallas_call | solution.py:107
  222.5 4.1 %fusion.48 = f32[512,256]{1,0:T(8,128)S(1)} fusion(bf16[512,4096]{1,0:T(8,128)(2,1)} %collective-permute-done.8, bf16[4096,256]{1,0:T(8,128)(2,1)} %bitcast.53), kind=kOutput, calls=%fused_computation.107 | convolution fusion | flops 1073741824 | bytes 6815744 | tf_op jit(solution)/shard_map/dot_general | solution.py:195
  226.6 2.0 fusion.1
  (92 shorter events, 25.6 us)
Async XLA Ops:
  7.2 196.0 %all-gather.2.cloned.1.call-start = ((), (), s32[]{:S(2)}) async-start(), calls=%async_computation | async-start | bytes 4718592 | tf_op jit(solution)/shard_map/all_gather | solution.py:194
  9.5 26.0 %collective-permute-start = (bf16[1280,256]{1,0:T(8,128)(2,1)S(1)}, bf16[1280,256]{1,0:T(8,128)(2,1)}, u32[]{:S(2)}, u32[]{:S(2)}) collective-permute-start(bf16[1280,256]{1,0:T(8,128)(2,1)S(1)} %pad_maximum_fusion.2), channel_id=1, source_target_pairs={{0,32},{32,64},{64,96},{96,128},{128,160},{160,192},{192,224},{224... | collective-permute-start | bytes 1966088 | tf_op jit(solution)/shard_map/ppermute | solution.py:132
  13.2 45.8 %collective-permute-start.1 = (bf16[1280,256]{1,0:T(8,128)(2,1)S(1)}, bf16[1280,256]{1,0:T(8,128)(2,1)}, u32[]{:S(2)}, u32[]{:S(2)}) collective-permute-start(bf16[1280,256]{1,0:T(8,128)(2,1)S(1)} %pad_maximum_fusion.2), channel_id=1, source_target_pairs={{0,64},{32,96},{64,128},{96,160},{128,192},{160,224},{192,0},{224,... | collective-permute-start | bytes 1966088 | tf_op jit(solution)/shard_map/ppermute | solution.py:132
  14.5 46.5 %collective-permute-start.2 = (bf16[1280,256]{1,0:T(8,128)(2,1)S(1)}, bf16[1280,256]{1,0:T(8,128)(2,1)S(1)}, u32[]{:S(2)}, u32[]{:S(2)}) collective-permute-start(bf16[1280,256]{1,0:T(8,128)(2,1)S(1)} %pad_maximum_fusion.2), channel_id=1, source_target_pairs={{0,96},{32,128},{64,160},{96,192},{128,224},{160,0},{192,32},{224,... | collective-permute-start | bytes 1966088 | tf_op jit(solution)/shard_map/ppermute | solution.py:132
  16.4 57.6 %collective-permute-start.3 = (bf16[1280,256]{1,0:T(8,128)(2,1)S(1)}, bf16[1280,256]{1,0:T(8,128)(2,1)S(1)}, u32[]{:S(2)}, u32[]{:S(2)}) collective-permute-start(bf16[1280,256]{1,0:T(8,128)(2,1)S(1)} %pad_maximum_fusion.2), channel_id=1, source_target_pairs={{0,128},{32,160},{64,192},{96,224},{128,0},{160,32},{192,64},{224,... | collective-permute-start | bytes 1966088 | tf_op jit(solution)/shard_map/ppermute | solution.py:132
  18.0 57.0 %collective-permute-start.4 = (bf16[1280,256]{1,0:T(8,128)(2,1)S(1)}, bf16[1280,256]{1,0:T(8,128)(2,1)S(1)}, u32[]{:S(2)}, u32[]{:S(2)}) collective-permute-start(bf16[1280,256]{1,0:T(8,128)(2,1)S(1)} %pad_maximum_fusion.2), channel_id=1, source_target_pairs={{0,160},{32,192},{64,224},{96,0},{128,32},{160,64},{192,96},{224,1... | collective-permute-start | bytes 1966088 | tf_op jit(solution)/shard_map/ppermute | solution.py:132
  23.4 9.9 %copy-start.9 = (pred[512]{0:T(512)(128)(4,1)}, pred[512]{0:T(512)(128)(4,1)S(1)}, u32[]{:S(2)}) copy-start(pred[512]{0:T(512)(128)(4,1)S(1)} %get-tuple-element.20) | copy-start | bytes 1540
  23.4 54.3 %copy-start.11 = (pred[512]{0:T(512)(128)(4,1)}, pred[512]{0:T(512)(128)(4,1)S(1)}, u32[]{:S(2)}) copy-start(pred[512]{0:T(512)(128)(4,1)S(1)} %get-tuple-element.21) | copy-start | bytes 1540
  23.4 54.2 %copy-start.13 = (pred[512]{0:T(512)(128)(4,1)}, pred[512]{0:T(512)(128)(4,1)S(1)}, u32[]{:S(2)}) copy-start(pred[512]{0:T(512)(128)(4,1)S(1)} %get-tuple-element.25) | copy-start | bytes 1540
  23.4 54.2 %copy-start.17 = (pred[512]{0:T(512)(128)(4,1)}, pred[512]{0:T(512)(128)(4,1)S(1)}, u32[]{:S(2)}) copy-start(pred[512]{0:T(512)(128)(4,1)S(1)} %get-tuple-element.24) | copy-start | bytes 1540
  28.2 51.5 %copy-start.3 = (s32[512]{0:T(512)}, s32[512]{0:T(512)S(1)}, u32[]{:S(2)}) copy-start(s32[512]{0:T(512)S(1)} %get-tuple-element.22) | copy-start | bytes 6148
  28.2 51.5 %copy-start.5 = (s32[512]{0:T(512)}, s32[512]{0:T(512)S(1)}, u32[]{:S(2)}) copy-start(s32[512]{0:T(512)S(1)} %get-tuple-element.23) | copy-start | bytes 6148
  35.6 40.3 %collective-permute-start.5 = (bf16[1280,256]{1,0:T(8,128)(2,1)S(1)}, bf16[1280,256]{1,0:T(8,128)(2,1)S(1)}, u32[]{:S(2)}, u32[]{:S(2)}) collective-permute-start(bf16[1280,256]{1,0:T(8,128)(2,1)S(1)} %pad_maximum_fusion.2), channel_id=1, source_target_pairs={{0,192},{32,224},{64,0},{96,32},{128,64},{160,96},{192,128},{224,1... | collective-permute-start | bytes 1966088 | tf_op jit(solution)/shard_map/ppermute | solution.py:132
  59.0 17.7 %collective-permute-start.6 = (bf16[1280,256]{1,0:T(8,128)(2,1)S(1)}, bf16[1280,256]{1,0:T(8,128)(2,1)S(1)}, u32[]{:S(2)}, u32[]{:S(2)}) collective-permute-start(bf16[1280,256]{1,0:T(8,128)(2,1)S(1)} %pad_maximum_fusion.2), channel_id=1, source_target_pairs={{0,224},{32,0},{64,32},{96,64},{128,96},{160,128},{192,160},{224,1... | collective-permute-start | bytes 1966088 | tf_op jit(solution)/shard_map/ppermute | solution.py:132
  88.2 8.7 %copy-start.6 = (s32[512]{0:T(512)S(1)}, s32[512]{0:T(512)}, u32[]{:S(2)}) copy-start(s32[512]{0:T(512)} %copy-done.5) | copy-start | bytes 6148
  88.2 8.7 %copy-start.10 = (pred[512]{0:T(512)(128)(4,1)S(1)}, pred[512]{0:T(512)(128)(4,1)}, u32[]{:S(2)}) copy-start(pred[512]{0:T(512)(128)(4,1)} %copy-done.9) | copy-start | bytes 1540
  88.2 8.7 %copy-start.12 = (pred[512]{0:T(512)(128)(4,1)S(1)}, pred[512]{0:T(512)(128)(4,1)}, u32[]{:S(2)}) copy-start(pred[512]{0:T(512)(128)(4,1)} %copy-done.11) | copy-start | bytes 1540
  88.2 8.7 %copy-start.14 = (pred[512]{0:T(512)(128)(4,1)S(1)}, pred[512]{0:T(512)(128)(4,1)}, u32[]{:S(2)}) copy-start(pred[512]{0:T(512)(128)(4,1)} %copy-done.13) | copy-start | bytes 1540
  88.2 8.7 %copy-start.18 = (pred[512]{0:T(512)(128)(4,1)S(1)}, pred[512]{0:T(512)(128)(4,1)}, u32[]{:S(2)}) copy-start(pred[512]{0:T(512)(128)(4,1)} %copy-done.17) | copy-start | bytes 1540
  116.8 10.9 %copy-start.1 = (s32[256]{0:T(256)S(1)}, s32[256]{0:T(256)}, u32[]{:S(2)}) copy-start(s32[256]{0:T(256)} %get-tuple-element.26) | copy-start | bytes 3076
  116.8 10.9 %copy-start.2 = (s32[256]{0:T(256)S(1)}, s32[256]{0:T(256)}, u32[]{:S(2)}) copy-start(s32[256]{0:T(256)} %get-tuple-element.27) | copy-start | bytes 3076
  116.8 10.9 %copy-start.15 = (pred[256]{0:T(512)(128)(4,1)S(1)}, pred[256]{0:T(512)(128)(4,1)}, u32[]{:S(2)}) copy-start(pred[256]{0:T(512)(128)(4,1)} %compare_and_fusion) | copy-start | bytes 772
  131.9 5.3 %collective-permute-start.7 = (bf16[512,256]{1,0:T(8,128)(2,1)S(1)}, bf16[512,256]{1,0:T(8,128)(2,1)S(1)}, u32[]{:S(2)}, u32[]{:S(2)}) collective-permute-start(bf16[512,256]{1,0:T(8,128)(2,1)S(1)} %fusion.16), channel_id=1, source_target_pairs={{0,2},{2,0},{1,3},{3,1},{4,6},{6,4},{5,7},{7,5},{8,10},{10,8},{9,1... | collective-permute-start | bytes 786440 | tf_op jit(solution)/shard_map/ppermute | solution.py:114
  203.1 19.4 %collective-permute-start.8 = (bf16[512,4096]{1,0:T(8,128)(2,1)}, bf16[512,4096]{1,0:T(8,128)(2,1)}, u32[]{:S(2)}, u32[]{:S(2)}) collective-permute-start(bf16[512,4096]{1,0:T(8,128)(2,1)} %all-gather.2.cloned.1.call-done), channel_id=1, source_target_pairs={{0,1},{1,0},{2,3},{3,2},{4,5},{5,4},{6,7},{7,6},{8,9},{9,8},{10,11... | collective-permute-start | bytes 12582920 | tf_op jit(solution)/shard_map/ppermute | solution.py:114
  (5 other events, 25.4 us)
Sparse Core Ops, SparseCore 0:
  138.3 64.8 all-gather.1

commit v3 on v2

--- a/solution.py
+++ b/solution.py
@@ -37,7 +37,7 @@
     return jnp.where(cols_idx == half, parity, table)
 
 
-def products(seg2d, span2d, lag_idx, lag_ok, n_targets, width, kt=32):
+def products(seg2d, span2d, lag_idx, lag_ok, n_targets, width, kt=128):
     half = seg2d.shape[0] // 2
     n_slots = span2d.shape[1] // width
     steps = half // kt
@@ -184,6 +184,7 @@
     rows = count_z * 2 * width
     w_own = lax.dynamic_index_in_dim(w5, core, axis=2, keepdims=False).reshape(rows, -1)
     w_other = lax.dynamic_index_in_dim(w5, 1 - core, axis=2, keepdims=False).reshape(rows, -1)
+    w_partner = swap(w_other, "core")
 
     other = swap(mixed, "xlo")
     pair = jnp.where(
@@ -192,9 +193,8 @@
         jnp.concatenate([other, mixed], axis=1),
     )
     ring = lax.all_gather(pair, "z", axis=1, tiled=True)
-    summed = jnp.dot(ring, w_own, preferred_element_type=jnp.float32) + jnp.dot(
-        swap(ring, "core"), w_other, preferred_element_type=jnp.float32
-    )
+    for_partner = jnp.dot(ring, w_partner, preferred_element_type=jnp.float32)
+    summed = jnp.dot(ring, w_own, preferred_element_type=jnp.float32) + swap(for_partner, "core")
     projected = summed.astype(jnp.bfloat16)
     return (projected, tail)
 

time: 236 us -> 227 us (0.962)
  waiting for transfers between devices: 102 us -> 89.8 us
  starting transfers between devices: 15.3 us -> 23.4 us
  Pallas kernels: 20.4 us -> 14.5 us
  matrix products: 28.6 us -> 31.6 us
    all_gather x1, waiting for transfers between devices: 65 us -> 50.6 us  [layer(): ring = lax.all_gather(pair, 'z', axis=1, tiled=True)]
    ppermute x2 -> x3, starting transfers between devices: 1.3 us -> 9.34 us  [swap(): return lax.ppermute(x, axis, [(i, (i + 1) % count) for i in range(count)])]
    pallas_call x2, Pallas kernels: 20.4 us -> 14.5 us  [products(): pl.pallas_call(kernel, grid_spec=grid_spec, out_shape=out_shape)]
    ppermute x2 -> x3, waiting for transfers between devices: 4.85 us -> 6.6 us  [swap(): return lax.ppermute(x, axis, [(i, (i + 1) % count) for i in range(count)])]
    unnamed x44 -> x42, local copies, waits for them, and re-layouts: 7.56 us -> 7.56 us
  transfers between devices with their start and end apart: 10 -> 11, of which waited for: 4 -> 5; matrix products, arithmetic and copies ran while one was open for 12% -> 12% of each run, Pallas kernels for 4% -> 3%
where the time goes in v3:
time: 227 us; the launch traced here: 226 us
  waiting for transfers between devices  89.8 us (40%)
  matrix products  31.6 us (14%)
  local copies, waits for them, and re-layouts  31.4 us (14%)
  starting transfers between devices  23.4 us (10%)
  other arithmetic  20.8 us (9%)
  between operations  15 us (7%)
  Pallas kernels  14.5 us (6%)
    all_gather x1, waiting for transfers between devices, layer(): ring = lax.all_gather(pair, 'z', axis=1, tiled=True)  50.6 us
    ppermute x7, waiting for transfers between devices, layer(): lax.ppermute(own, 'ctx', [(i, (i + shift) % cycle_size) for i in range(cy...  32.6 us
    pallas_call x2, Pallas kernels, products(): pl.pallas_call(kernel, grid_spec=grid_spec, out_shape=out_shape)  14.5 us
    ppermute x7, starting transfers between devices, layer(): lax.ppermute(own, 'ctx', [(i, (i + shift) % cycle_size) for i in range(cy...  14 us
    dot_general x1, matrix products, layer(): jnp.dot(forward, seg_time, preferred_element_type=jnp.float32)  12.5 us
    ppermute x3, starting transfers between devices, swap(): return lax.ppermute(x, axis, [(i, (i + 1) % count) for i in range(count)])  9.34 us
    concatenate x2, local copies, waits for them, and re-layouts, layer(): jnp.concatenate([blocks.transpose(2, 0, 1, 3), jnp.zeros((1, cycle_size,...  8.71 us
    unnamed x42, local copies, waits for them, and re-layouts  7.56 us
  transfers between devices with their start and end apart: 11, of which 5 were waited for; matrix products, arithmetic and copies ran while one was open for 12% of the time, Pallas kernels for 3%

profile of v3, /device:TPU:1, one launch (start us, length us, event | category | flops | bytes accessed | tf_op | source)
XLA Modules:
  0.0 226.5 jit_solution(12056067196292972833)
XLA Ops:
  9.5 3.6 %collective-permute-start = (bf16[1280,256]{1,0:T(8,128)(2,1)S(1)}, bf16[1280,256]{1,0:T(8,128)(2,1)}, u32[]{:S(2)}, u32[]{:S(2)}) collective-permute-start(bf16[1280,256]{1,0:T(8,128)(2,1)S(1)} %pad_maximum_fusion.2), channel_id=1, source_target_pairs={{0,32},{32,64},{64,96},{96,128},{128,160},{160,192},{192,224},{224... | collective-permute-start | bytes 1966088 | tf_op jit(solution)/shard_map/ppermute | solution.py:132
  18.0 4.5 %collective-permute-start.4 = (bf16[1280,256]{1,0:T(8,128)(2,1)S(1)}, bf16[1280,256]{1,0:T(8,128)(2,1)S(1)}, u32[]{:S(2)}, u32[]{:S(2)}) collective-permute-start(bf16[1280,256]{1,0:T(8,128)(2,1)S(1)} %pad_maximum_fusion.2), channel_id=1, source_target_pairs={{0,160},{32,192},{64,224},{96,0},{128,32},{160,64},{192,96},{224,1... | collective-permute-start | bytes 1966088 | tf_op jit(solution)/shard_map/ppermute | solution.py:132
  28.2 5.0 %select_convert_fusion = bf16[512,512]{1,0:T(8,128)(2,1)S(1)} fusion(s32[512]{0:T(512)S(1)} %get-tuple-element.18, s32[512]{0:T(512)S(1)} %get-tuple-element.19, s32[512]{0:T(512)S(1)} %get-tuple-element.22, s32[512]{0:T(512)S(1)} %get-tuple-element.23, pred[512]{0:T(512)(128)(4,1)S(1)} %get-tuple-element.25, pred[512]{0:T(512)(128)(4,1)S(1)} %get-tuple-element.20, ...), kind=kLoop, calls=%fused_computation.19 | loop fusion | flops 6029312 | bytes 534528 | tf_op jit(solution)/shard_map/convert_element_type | solution.py:126
  36.6 2.0 bitcast_dynamic-update-slice_fusion.6
  38.6 20.4 %collective-permute-done.1 = bf16[1280,256]{1,0:T(8,128)(2,1)} collective-permute-done((bf16[1280,256]{1,0:T(8,128)(2,1)S(1)}, bf16[1280,256]{1,0:T(8,128)(2,1)}, u32[]{:S(2)}, u32[]{:S(2)}) %collective-permute-start.1) | collective-permute-done | bytes 655392 | tf_op jit(solution)/shard_map/ppermute | solution.py:132
  59.0 2.0 bitcast_dynamic-update-slice_fusion.5
  61.9 12.2 %collective-permute-done.3 = bf16[1280,256]{1,0:T(8,128)(2,1)S(1)} collective-permute-done((bf16[1280,256]{1,0:T(8,128)(2,1)S(1)}, bf16[1280,256]{1,0:T(8,128)(2,1)S(1)}, u32[]{:S(2)}, u32[]{:S(2)}) %collective-permute-start.3) | collective-permute-done | bytes 655392 | tf_op jit(solution)/shard_map/ppermute | solution.py:132
  77.6 2.1 slice.59
  82.0 2.0 fusion
  84.0 4.2 %pad_maximum_fusion = bf16[512,8,3,256]{3,0,2,1:T(8,128)(2,1)} fusion(bf16[255,8,3,256]{3,0,2,1:T(8,128)(2,1)S(1)} %fusion, bf16[256,8,3,256]{3,0,2,1:T(8,128)(2,1)S(1)} %bitcast.47, bf16[512]{0:T(512)(128)(2,1)S(1)} %pad.11.clone), kind=kLoop, calls=%fused_computation.2 | loop fusion | flops 18874368 | bytes 12571648 | tf_op jit(solution)/shard_map/concatenate | solution.py:146
  88.2 8.7 %copy.10 = bf16[512,8,3,256]{0,3,2,1:T(8,128)(2,1)} copy(bf16[512,8,3,256]{3,0,2,1:T(8,128)(2,1)} %pad_maximum_fusion) | data formatting | bytes 12582912 | tf_op jit(solution)/shard_map/concatenate | solution.py:146
  96.9 12.5 %convolution_convert_fusion.seg_re.seg_im = bf16[512,6144]{1,0:T(8,128)(2,1)} fusion(bf16[512,6144]{0,1:T(8,128)(2,1)} %bitcast.50, s32[512]{0:T(512)S(1)} %get-tuple-element.18, s32[512]{0:T(512)S(1)} %get-tuple-element.19, s32[512]{0:T(512)S(1)} %copy-done.4, s32[512]{0:T(512)S(1)} %copy-done.6, pred[512]{0:T(512)(128)(4,1)S(1)} %copy-done.14, ...), kind=kOutput, calls=%fused_computation.1 | convolution fusion | flops 3230400512 | bytes 12593152 | tf_op jit(solution)/shard_map/dot_general | solution.py:154
  109.4 2.4 %copy.11 = bf16[256,8,2,256]{0,3,2,1:T(8,128)(2,1)} copy(bf16[256,8,2,256]{3,0,2,1:T(8,128)(2,1)S(1)} %bitcast.48) | data formatting | bytes 4194304 | tf_op jit(solution)/shard_map/transpose | solution.py:155
  111.8 5.0 %convolution_convert_fusion.1.sp_re.sp_im = bf16[512,4096]{1,0:T(8,128)(2,1)} fusion(bf16[256,4096]{0,1:T(8,128)(2,1)} %bitcast.49, bf16[512,512]{1,0:T(8,128)(2,1)S(1)} %select_convert_fusion), kind=kOutput, calls=%fused_computation.3 | convolution fusion | flops 1075838976 | bytes 6553600 | tf_op jit(solution)/shard_map/dot_general | solution.py:156
  116.8 7.5 %shard_map.95 = (f32[256,512]{1,0:T(8,128)}, f32[256,512]{1,0:T(8,128)}) custom-call(s32[32]{0:T(128)} %reshape.173.lag_ref, s32[32]{0:T(128)} %reshape.174.ok_ref, bf16[512,6144]{1,0:T(8,128)(2,1)} %convolution_convert_fusion.seg_re.seg_im, bf16[512,6144]{1,0:T(8,128)(2,1)} %convolution_convert_fusion.seg_re.seg_im, ...), custom_call_target="tpu_custom_call" | custom-call | tf_op jit(solution)/shard_map/pallas_call | solution.py:107
  124.3 4.0 %fusion.5 = f32[256,512]{1,0:T(8,128)S(1)} fusion(f32[256,512]{1,0:T(8,128)} %get-tuple-element.9, f32[256,512]{1,0:T(8,128)} %get-tuple-element.8, s32[512]{0:T(512)S(1)} %get-tuple-element.18, s32[512]{0:T(512)S(1)} %get-tuple-element.19, s32[256]{0:T(256)S(1)} %copy-done.1, s32[256]{0:T(256)S(1)} %copy-done.2, pred[256]{0:T(512)(128)(4,1)S(1)} %copy-done.15, ...), kind=kOutput, calls=%fused_computation.15 | convolution fusion | flops 406454272 | bytes 1580800 | tf_op jit(solution)/shard_map/dot_general | solution.py:171
  129.0 4.9 %collective-permute-done.7 = bf16[512,256]{1,0:T(8,128)(2,1)S(1)} collective-permute-done((bf16[512,256]{1,0:T(8,128)(2,1)S(1)}, bf16[512,256]{1,0:T(8,128)(2,1)S(1)}, u32[]{:S(2)}, u32[]{:S(2)}) %collective-permute-start.7) | collective-permute-done | bytes 262176 | tf_op jit(solution)/shard_map/ppermute | solution.py:114
  134.8 2.6 %constant_dynamic-slice_fusion.1 = (bf16[8,2,1,256,256]{4,3,2,1,0:T(8,128)(2,1)S(1)}, bf16[8,2,1,256,256]{4,3,2,1,0:T(8,128)(2,1)S(1)}) fusion(bf16[8,2,2,256,256]{4,3,2,1,0:T(8,128)(2,1)} %bitcast.51, s32[]{:T(128)S(6)} %select_n.187, s32[]{:T(128)S(6)} %select_n.188), kind=kLoop, calls=%fused_computation.104 | loop fusion | bytes 8388616 | tf_op jit(solution)/shard_map/jit(dynamic_index_in_dim)/dynamic_slice | solution.py:185
  137.4 8.0 %collective-permute-start.8 = (bf16[4096,256]{1,0:T(8,128)(2,1)S(1)}, bf16[4096,256]{1,0:T(8,128)(2,1)}, u32[]{:S(2)}, u32[]{:S(2)}) collective-permute-start(bf16[4096,256]{1,0:T(8,128)(2,1)S(1)} %bitcast.53), channel_id=1, source_target_pairs={{0,1},{1,0},{2,3},{3,2},{4,5},{5,4},{6,7},{7,6},{8,9},{9,8},{10,11... | collective-permute-start | bytes 6291464 | tf_op jit(solution)/shard_map/ppermute | solution.py:114
  145.4 2.2 fusion.10
  149.3 50.6 %all-gather.2.cloned.1.call-done = bf16[512,4096]{1,0:T(8,128)(2,1)} async-done(((bf16[512,512]{1,0:T(8,128)(2,1)}), bf16[512,4096]{1,0:T(8,128)(2,1)}) %all-gather.2.cloned.1.call-update) | async-done | bytes 4194320 | tf_op jit(solution)/shard_map/all_gather | solution.py:195
  200.0 4.9 %fusion.48 = f32[512,256]{1,0:T(8,128)} fusion(bf16[512,4096]{1,0:T(8,128)(2,1)} %all-gather.2.cloned.1.call-done, bf16[4096,256]{1,0:T(8,128)(2,1)} %collective-permute-done.8), kind=kOutput, calls=%fused_computation.107 | convolution fusion | flops 1073741824 | bytes 6815744 | tf_op jit(solution)/shard_map/dot_general | solution.py:196
  206.3 7.0 %shard_map.96 = (f32[256,256]{1,0:T(8,128)}, f32[256,256]{1,0:T(8,128)}) custom-call(s32[16]{0:T(128)} %get-tuple-element.29.lag_ref, s32[16]{0:T(128)} %get-tuple-element.28.ok_ref, bf16[512,6144]{1,0:T(8,128)(2,1)} %convolution_convert_fusion.seg_re.seg_im, bf16[512,6144]{1,0:T(8,128)(2,1)} %convolution_convert_fusion.seg_re.seg_im, ...), custom_call_target="tpu_custom_call" | custom-call | tf_op jit(solution)/shard_map/pallas_call | solution.py:107
  215.5 4.1 %fusion.1 = bf16[512,256]{1,0:T(8,128)(2,1)} fusion(f32[512,256]{1,0:T(8,128)S(1)} %collective-permute-done.9, bf16[512,4096]{1,0:T(8,128)(2,1)} %all-gather.2.cloned.1.call-done, bf16[4096,256]{1,0:T(8,128)(2,1)S(1)} %bitcast.52), kind=kOutput, calls=%fused_computation.10 | convolution fusion | flops 1074003968 | bytes 7077888 | tf_op jit(solution)/shard_map/dot_general | solution.py:197
  (92 shorter events, 29.1 us)
Async XLA Ops:
  7.2 192.8 %all-gather.2.cloned.1.call-start = ((), (), s32[]{:S(2)}) async-start(), calls=%async_computation | async-start | bytes 4718592 | tf_op jit(solution)/shard_map/all_gather | solution.py:195
  9.5 26.0 %collective-permute-start = (bf16[1280,256]{1,0:T(8,128)(2,1)S(1)}, bf16[1280,256]{1,0:T(8,128)(2,1)}, u32[]{:S(2)}, u32[]{:S(2)}) collective-permute-start(bf16[1280,256]{1,0:T(8,128)(2,1)S(1)} %pad_maximum_fusion.2), channel_id=1, source_target_pairs={{0,32},{32,64},{64,96},{96,128},{128,160},{160,192},{192,224},{224... | collective-permute-start | bytes 1966088 | tf_op jit(solution)/shard_map/ppermute | solution.py:132
  13.2 45.8 %collective-permute-start.1 = (bf16[1280,256]{1,0:T(8,128)(2,1)S(1)}, bf16[1280,256]{1,0:T(8,128)(2,1)}, u32[]{:S(2)}, u32[]{:S(2)}) collective-permute-start(bf16[1280,256]{1,0:T(8,128)(2,1)S(1)} %pad_maximum_fusion.2), channel_id=1, source_target_pairs={{0,64},{32,96},{64,128},{96,160},{128,192},{160,224},{192,0},{224,... | collective-permute-start | bytes 1966088 | tf_op jit(solution)/shard_map/ppermute | solution.py:132
  14.5 46.5 %collective-permute-start.2 = (bf16[1280,256]{1,0:T(8,128)(2,1)S(1)}, bf16[1280,256]{1,0:T(8,128)(2,1)S(1)}, u32[]{:S(2)}, u32[]{:S(2)}) collective-permute-start(bf16[1280,256]{1,0:T(8,128)(2,1)S(1)} %pad_maximum_fusion.2), channel_id=1, source_target_pairs={{0,96},{32,128},{64,160},{96,192},{128,224},{160,0},{192,32},{224,... | collective-permute-start | bytes 1966088 | tf_op jit(solution)/shard_map/ppermute | solution.py:132
  16.4 57.6 %collective-permute-start.3 = (bf16[1280,256]{1,0:T(8,128)(2,1)S(1)}, bf16[1280,256]{1,0:T(8,128)(2,1)S(1)}, u32[]{:S(2)}, u32[]{:S(2)}) collective-permute-start(bf16[1280,256]{1,0:T(8,128)(2,1)S(1)} %pad_maximum_fusion.2), channel_id=1, source_target_pairs={{0,128},{32,160},{64,192},{96,224},{128,0},{160,32},{192,64},{224,... | collective-permute-start | bytes 1966088 | tf_op jit(solution)/shard_map/ppermute | solution.py:132
  18.0 57.0 %collective-permute-start.4 = (bf16[1280,256]{1,0:T(8,128)(2,1)S(1)}, bf16[1280,256]{1,0:T(8,128)(2,1)S(1)}, u32[]{:S(2)}, u32[]{:S(2)}) collective-permute-start(bf16[1280,256]{1,0:T(8,128)(2,1)S(1)} %pad_maximum_fusion.2), channel_id=1, source_target_pairs={{0,160},{32,192},{64,224},{96,0},{128,32},{160,64},{192,96},{224,1... | collective-permute-start | bytes 1966088 | tf_op jit(solution)/shard_map/ppermute | solution.py:132
  23.4 9.9 %copy-start.9 = (pred[512]{0:T(512)(128)(4,1)}, pred[512]{0:T(512)(128)(4,1)S(1)}, u32[]{:S(2)}) copy-start(pred[512]{0:T(512)(128)(4,1)S(1)} %get-tuple-element.20) | copy-start | bytes 1540
  23.4 54.3 %copy-start.11 = (pred[512]{0:T(512)(128)(4,1)}, pred[512]{0:T(512)(128)(4,1)S(1)}, u32[]{:S(2)}) copy-start(pred[512]{0:T(512)(128)(4,1)S(1)} %get-tuple-element.21) | copy-start | bytes 1540
  23.4 54.2 %copy-start.13 = (pred[512]{0:T(512)(128)(4,1)}, pred[512]{0:T(512)(128)(4,1)S(1)}, u32[]{:S(2)}) copy-start(pred[512]{0:T(512)(128)(4,1)S(1)} %get-tuple-element.25) | copy-start | bytes 1540
  23.4 54.2 %copy-start.16 = (pred[512]{0:T(512)(128)(4,1)}, pred[512]{0:T(512)(128)(4,1)S(1)}, u32[]{:S(2)}) copy-start(pred[512]{0:T(512)(128)(4,1)S(1)} %get-tuple-element.24) | copy-start | bytes 1540
  28.2 51.5 %copy-start.3 = (s32[512]{0:T(512)}, s32[512]{0:T(512)S(1)}, u32[]{:S(2)}) copy-start(s32[512]{0:T(512)S(1)} %get-tuple-element.22) | copy-start | bytes 6148
  28.2 51.5 %copy-start.5 = (s32[512]{0:T(512)}, s32[512]{0:T(512)S(1)}, u32[]{:S(2)}) copy-start(s32[512]{0:T(512)S(1)} %get-tuple-element.23) | copy-start | bytes 6148
  35.6 40.3 %collective-permute-start.5 = (bf16[1280,256]{1,0:T(8,128)(2,1)S(1)}, bf16[1280,256]{1,0:T(8,128)(2,1)S(1)}, u32[]{:S(2)}, u32[]{:S(2)}) collective-permute-start(bf16[1280,256]{1,0:T(8,128)(2,1)S(1)} %pad_maximum_fusion.2), channel_id=1, source_target_pairs={{0,192},{32,224},{64,0},{96,32},{128,64},{160,96},{192,128},{224,1... | collective-permute-start | bytes 1966088 | tf_op jit(solution)/shard_map/ppermute | solution.py:132
  59.0 17.7 %collective-permute-start.6 = (bf16[1280,256]{1,0:T(8,128)(2,1)S(1)}, bf16[1280,256]{1,0:T(8,128)(2,1)S(1)}, u32[]{:S(2)}, u32[]{:S(2)}) collective-permute-start(bf16[1280,256]{1,0:T(8,128)(2,1)S(1)} %pad_maximum_fusion.2), channel_id=1, source_target_pairs={{0,224},{32,0},{64,32},{96,64},{128,96},{160,128},{192,160},{224,1... | collective-permute-start | bytes 1966088 | tf_op jit(solution)/shard_map/ppermute | solution.py:132
  88.2 8.7 %copy-start.4 = (s32[512]{0:T(512)S(1)}, s32[512]{0:T(512)}, u32[]{:S(2)}) copy-start(s32[512]{0:T(512)} %copy-done.3) | copy-start | bytes 6148
  88.2 8.7 %copy-start.6 = (s32[512]{0:T(512)S(1)}, s32[512]{0:T(512)}, u32[]{:S(2)}) copy-start(s32[512]{0:T(512)} %copy-done.5) | copy-start | bytes 6148
  88.2 8.7 %copy-start.10 = (pred[512]{0:T(512)(128)(4,1)S(1)}, pred[512]{0:T(512)(128)(4,1)}, u32[]{:S(2)}) copy-start(pred[512]{0:T(512)(128)(4,1)} %copy-done.9) | copy-start | bytes 1540
  88.2 8.7 %copy-start.12 = (pred[512]{0:T(512)(128)(4,1)S(1)}, pred[512]{0:T(512)(128)(4,1)}, u32[]{:S(2)}) copy-start(pred[512]{0:T(512)(128)(4,1)} %copy-done.11) | copy-start | bytes 1540
  88.2 8.7 %copy-start.14 = (pred[512]{0:T(512)(128)(4,1)S(1)}, pred[512]{0:T(512)(128)(4,1)}, u32[]{:S(2)}) copy-start(pred[512]{0:T(512)(128)(4,1)} %copy-done.13) | copy-start | bytes 1540
  88.2 8.7 %copy-start.17 = (pred[512]{0:T(512)(128)(4,1)S(1)}, pred[512]{0:T(512)(128)(4,1)}, u32[]{:S(2)}) copy-start(pred[512]{0:T(512)(128)(4,1)} %copy-done.16) | copy-start | bytes 1540
  116.8 7.6 %copy-start.15 = (pred[256]{0:T(512)(128)(4,1)S(1)}, pred[256]{0:T(512)(128)(4,1)}, u32[]{:S(2)}) copy-start(pred[256]{0:T(512)(128)(4,1)} %compare_and_fusion) | copy-start | bytes 772
  128.5 5.3 %collective-permute-start.7 = (bf16[512,256]{1,0:T(8,128)(2,1)S(1)}, bf16[512,256]{1,0:T(8,128)(2,1)S(1)}, u32[]{:S(2)}, u32[]{:S(2)}) collective-permute-start(bf16[512,256]{1,0:T(8,128)(2,1)S(1)} %fusion.16), channel_id=1, source_target_pairs={{0,2},{2,0},{1,3},{3,1},{4,6},{6,4},{5,7},{7,5},{8,10},{10,8},{9,1... | collective-permute-start | bytes 786440 | tf_op jit(solution)/shard_map/ppermute | solution.py:114
  137.4 12.0 %collective-permute-start.8 = (bf16[4096,256]{1,0:T(8,128)(2,1)S(1)}, bf16[4096,256]{1,0:T(8,128)(2,1)}, u32[]{:S(2)}, u32[]{:S(2)}) collective-permute-start(bf16[4096,256]{1,0:T(8,128)(2,1)S(1)} %bitcast.53), channel_id=1, source_target_pairs={{0,1},{1,0},{2,3},{3,2},{4,5},{5,4},{6,7},{7,6},{8,9},{9,8},{10,11... | collective-permute-start | bytes 6291464 | tf_op jit(solution)/shard_map/ppermute | solution.py:114
  204.9 10.6 %collective-permute-start.9 = (f32[512,256]{1,0:T(8,128)}, f32[512,256]{1,0:T(8,128)S(1)}, u32[]{:S(2)}, u32[]{:S(2)}) collective-permute-start(f32[512,256]{1,0:T(8,128)} %fusion.48), channel_id=1, source_target_pairs={{0,1},{1,0},{2,3},{3,2},{4,5},{5,4},{6,7},{7,6},{8,9},{9,8},{10,11... | collective-permute-start | bytes 1572872 | tf_op jit(solution)/shard_map/ppermute | solution.py:114
  (5 other events, 25.3 us)
Sparse Core Ops, SparseCore 0:
  134.9 65.0 all-gather.1
